TPU v7x, 32 devices: a whole 2x2x4 slice. The times are simulated.
32 devices in a mesh: dp: 2 (over x), mp: 16 (over z, y, core).
Axes of the slice: x: 2, y: 2, z: 4, core: 2. Of those that a mesh axis runs over, the one named last changes fastest.
Arguments:
- node_features: bfloat16 [512, 6144], P('mp', 'dp'), may hold values from -6 to 6
- weights_one: bfloat16 [1024, 512], replicated, may hold values from -0.25 to 0.25
- weights_two: bfloat16 [1024, 512], replicated, may hold values from -0.25 to 0.25
- neighbor_owner: int32 [6144, 8], P('dp'), may hold values from 0 to 15, all different within a row; in each aligned block of 192 rows (0 to 191, 192 to 383, ...) at most 144 rows name the same one
- neighbor_row: int32 [6144, 8], P('dp'), may hold values from 0 to 191
- neighbor_count: int32 [6144], P('dp'), may hold values from 4 to 8
- cotangent: bfloat16 [6144, 512], P(('dp', 'mp')), may hold values from -0.076171875 to 0.076171875
Outputs:
- node_output: bfloat16 [6144, 512], P(('dp', 'mp'))
- weight_grads: float32 [2048, 512], P(('dp', 'mp'))
Inputs may be any that keep to these rules, and one draw needn't show every extreme that they name: `neighbor_owner`: each row names 8 different owners; among the rows of one device (aligned blocks of 192 rows) no owner is named more than 144 times, and in some block one owner exactly 144 times. Slots k >= neighbor_count[r] are padding and carry no edge.
All inputs are finite; a program needn't handle non-finite values.
Results may differ from a plain program's by a relative error of at most 0.0052.
Values may be sent and summed in bfloat16 or wider, within the bound.
No kernel may reach another device: no remote copies, remote signals or barrier semaphores. Data moves between devices by JAX's collectives and lax.ppermute only.
A program may use at most 64 MiB of HBM per device.

v0:
```python
import jax
import jax.numpy as jnp
from jax import lax
from jax.sharding import PartitionSpec as P


def column_mean(table, indices, live, inverse):
    total = jnp.zeros((table.shape[0], indices.shape[1]), jnp.float32)
    for slot_index in range(indices.shape[0]):
        picked = jnp.take(table, indices[slot_index], axis=1)
        kept = jnp.where(live[slot_index][None, :], picked, jnp.zeros_like(picked))
        total = total + kept.astype(jnp.float32)
    return (total * inverse[None, :]).astype(jnp.bfloat16)


def silu_slope(values):
    sigmoid = jax.nn.sigmoid(values)
    return sigmoid * (1.0 + values * (1.0 - sigmoid))


def contract(left, right, left_dim, right_dim):
    return lax.dot_general(
        left, right, (((left_dim,), (right_dim,)), ((), ())), preferred_element_type=jnp.float32
    )


def swap(values, axis, mask):
    size = lax.axis_size(axis)
    return lax.ppermute(values, axis, [(j, j ^ mask) for j in range(size)])


def halving_scatter(terms, order):
    n_mp = lax.axis_size("mp")
    top = n_mp.bit_length() - 1
    place = lax.axis_index("dp") * n_mp + lax.axis_index("mp")
    rows = terms.shape[0] // (2 * n_mp)
    bits = list(range(top, -1, -1))
    values = terms.reshape((2,) * (top + 1) + (rows, terms.shape[1]))
    for bit in order:
        position = bits.index(bit)
        mine = place >> bit & 1
        keep = lax.dynamic_index_in_dim(values, mine, position, keepdims=False)
        send = lax.dynamic_index_in_dim(values, 1 - mine, position, keepdims=False)
        got = swap(send, "dp", 1) if bit == top else swap(send, "mp", 1 << bit)
        values = keep + got
        bits.pop(position)
    return values.reshape(rows, terms.shape[1])


def doubling_step(current, order, step):
    own = lax.axis_index("mp")
    bit = order[step]
    got = swap(current, "mp", 1 << bit)
    low = jnp.where(own >> bit & 1 == 0, current, got)
    high = jnp.where(own >> bit & 1 == 0, got, current)
    return jnp.stack([low, high], axis=sum((1 for done in order[:step] if done > bit)))


def doubling_gather(rows, order):
    current = rows
    for step in range(len(order)):
        current = doubling_step(current, order, step)
    return current.reshape(-1, rows.shape[-1])


def split_gather(rows, order, other):
    if other == order:
        return doubling_gather(rows, order)
    half = rows.shape[1] // 2
    return jnp.concatenate(
        [doubling_gather(rows[:, :half], order), doubling_gather(rows[:, half:], other)], axis=1
    )


def shards(
    node_features, weights_one, weights_two, neighbor_owner, neighbor_row, neighbor_count, cotangent
):
    devices = lax.axis_size("mp")
    own_index = lax.axis_index("mp")
    node_dev = cotangent.shape[0]
    all_nodes = neighbor_owner.shape[0]
    fanout = neighbor_owner.shape[1]
    feat_width = weights_one.shape[0] // 2
    hidden = weights_one.shape[1]
    live = lax.broadcasted_iota(jnp.int32, (all_nodes, fanout), 1) < neighbor_count[:, None]
    inverse_all = 1.0 / neighbor_count.astype(jnp.float32)
    owner_ids = lax.broadcasted_iota(jnp.int32, (devices, 1, 1), 0)
    match = (neighbor_owner[None, :, :] == owner_ids) & live[None, :, :]
    rowsel = jnp.max(jnp.where(match, neighbor_row[None, :, :], -1), axis=2)
    self_two = weights_two[:hidden]
    neigh_two = weights_two[hidden:]
    own_inverse = lax.dynamic_slice_in_dim(inverse_all, own_index * node_dev, node_dev, 0)
    order = list(range(devices.bit_length() - 2, -1, -1))
    other = [1] + [bit for bit in order if bit != 1] if devices == 16 else order
    dense_one = all_nodes * all_nodes <= 4096 * 4096
    down_neigh = (contract(cotangent, neigh_two, 1, 1) * own_inverse[:, None]).astype(jnp.bfloat16)
    half = down_neigh.shape[1] // 2
    parts = [down_neigh[:, :half], down_neigh[:, half:]]
    orders = [order, other]
    steps_done = 0

    def advance(parts, steps_done):
        if steps_done < len(order):
            parts = [doubling_step(p, o, steps_done) for p, o in zip(parts, orders)]
        return (parts, steps_done + 1)

    parts, steps_done = advance(parts, steps_done)
    with jax.named_scope("layer_one_mean"):
        if dense_one:
            row_ids = lax.broadcasted_iota(jnp.int32, (1, node_dev, 1), 1)
            adjacency = (rowsel[:, None, :] == row_ids).astype(jnp.bfloat16)
            adjacency = adjacency.reshape(devices * node_dev, all_nodes)
            parts, adjacency = lax.optimization_barrier((parts, adjacency))
            parts, steps_done = advance(parts, steps_done)
            summed = contract(node_features, adjacency, 1, 0)
            agg_one_cols = (summed * inverse_all[None, :]).astype(jnp.bfloat16)
        else:
            owner_slots = neighbor_owner.T
            global_ids = owner_slots * node_dev + neighbor_row.T
            agg_one_cols = column_mean(node_features, global_ids, live.T, inverse_all)
    parts, agg_one_cols = lax.optimization_barrier((parts, agg_one_cols))
    parts, steps_done = advance(parts, steps_done)
    own_feats, own_agg_one = (
        lax.all_to_all(node_features, "mp", split_axis=1, concat_axis=0, tiled=True),
        lax.all_to_all(agg_one_cols, "mp", split_axis=1, concat_axis=0, tiled=True),
    )
    parts, own_agg_one = lax.optimization_barrier((parts, own_agg_one))
    with jax.named_scope("neighbor_tables"):
        row_ids = lax.broadcasted_iota(jnp.int32, (1, node_dev, 1), 1)
        own_sel = lax.dynamic_slice_in_dim(rowsel, own_index * node_dev, node_dev, 1)
        own_edges = (own_sel[:, None, :] == row_ids).astype(jnp.bfloat16)
        own_edges = own_edges.reshape(devices * node_dev, node_dev)
        mine_sel = lax.dynamic_index_in_dim(rowsel, own_index, 0, keepdims=False)
        named_by = (mine_sel[:, None] == row_ids.reshape(1, node_dev)).astype(jnp.bfloat16)
    pre_one = contract(own_feats, weights_one[:feat_width], 0, 0) + contract(
        own_agg_one, weights_one[feat_width:], 0, 0
    )
    hidden_one = jax.nn.silu(pre_one).astype(jnp.bfloat16)
    hparts = [hidden_one[:, :half], hidden_one[:, half:]]
    hparts = [doubling_step(p, o, 0) for p, o in zip(hparts, orders)]
    hparts, parts = lax.optimization_barrier((hparts, parts))
    while steps_done < len(order):
        parts, steps_done = advance(parts, steps_done)
    for step in range(1, len(order)):
        hparts = [doubling_step(p, o, step) for p, o in zip(hparts, orders)]
    hidden_all = jnp.concatenate([p.reshape(-1, half) for p in hparts], axis=1)
    down_all = jnp.concatenate([p.reshape(-1, half) for p in parts], axis=1)
    total = contract(own_edges, hidden_all, 0, 0)
    agg_two = (total * own_inverse[:, None]).astype(jnp.bfloat16)
    node_output = (
        contract(hidden_one, self_two, 1, 0) + contract(agg_two, neigh_two, 1, 0)
    ).astype(jnp.bfloat16)
    down_self = contract(cotangent, self_two, 1, 1)
    neighbor_sum = contract(named_by, down_all, 0, 0)
    grad_hidden = down_self + neighbor_sum
    grad_pre = (grad_hidden * silu_slope(pre_one)).astype(jnp.bfloat16)
    terms = jnp.concatenate(
        [
            contract(own_feats, grad_pre, 1, 0),
            contract(own_agg_one, grad_pre, 1, 0),
            contract(hidden_one, cotangent, 0, 0),
            contract(agg_two, cotangent, 0, 0),
        ],
        axis=0,
    )
    with jax.named_scope("weight_grad_sum"):
        if lax.axis_size("dp") == 2 and devices == 16:
            half = terms.shape[1] // 2
            weight_grads = jnp.concatenate(
                [
                    halving_scatter(terms[:, :half], [0, 4, 1, 3, 2]),
                    halving_scatter(terms[:, half:], [0, 1, 4, 2, 3]),
                ],
                axis=1,
            )
        else:
            weight_grads = lax.psum_scatter(terms, ("dp", "mp"), scatter_dimension=0, tiled=True)
    return (node_output, weight_grads)


def solution(mesh):
    in_specs = (
        P("mp", "dp"),
        P(),
        P(),
        P("dp", None),
        P("dp", None),
        P("dp"),
        P(("dp", "mp"), None),
    )
    out_specs = (P(("dp", "mp"), None), P(("dp", "mp"), None))
    return jax.shard_map(shards, mesh=mesh, in_specs=in_specs, out_specs=out_specs, check_vma=False)
```

profile of v0, /device:TPU:0, one launch (start us, length us, event | category | flops | bytes accessed | tf_op | source)
XLA Modules:
  0.0 135.3 jit_solution(17648339066246796679)
XLA Ops:
  0.7 0.8 convert_divide_fusion
  1.6 1.4 %fusion.21 = bf16[192,512]{1,0:T(8,128)(2,1)S(1)} fusion(bf16[192,512]{1,0:T(8,128)(2,1)S(1)} %copy-done, bf16[1024,512]{1,0:T(8,128)(2,1)} %param.9, f32[192]{0:T(256)S(1)} %dynamic_slice.78), kind=kOutput, calls=%fused_computation.33 | convolution fusion | flops 100859904 | bytes 918272 | tf_op jit(solution)/shard_map/dot_general | solution.py:22
  3.0 4.1 %collective-permute-start = (bf16[192,256]{1,0:T(8,128)(2,1)S(1)}, bf16[192,256]{1,0:T(8,128)(2,1)S(1)}, u32[]{:S(2)}, u32[]{:S(2)}) collective-permute-start(bf16[192,256]{1,0:T(8,128)(2,1)S(1)} %get-tuple-element.71), channel_id=1, source_target_pairs={{0,8},{1,9},{2,10},{3,11},{4,12},{5,13},{6,14},{7,15},{8,0},{9,1},... | collective-permute-start | bytes 294920 | tf_op jit(solution)/shard_map/ppermute | solution.py:29
  7.1 1.5 %collective-permute-start.1 = (bf16[192,256]{1,0:T(8,128)(2,1)S(1)}, bf16[192,256]{1,0:T(8,128)(2,1)S(1)}, u32[]{:S(2)}, u32[]{:S(2)}) collective-permute-start(bf16[192,256]{1,0:T(8,128)(2,1)S(1)} %get-tuple-element.70), channel_id=1, source_target_pairs={{0,2},{1,3},{2,0},{3,1},{4,6},{5,7},{6,4},{7,5},{8,10},{9,11},{10,... | collective-permute-start | bytes 294920 | tf_op jit(solution)/shard_map/ppermute | solution.py:29
  8.6 1.2 all_to_all.28
  9.8 0.8 copy.29
  10.6 3.5 %all-to-all-start = ((bf16[32,16,192]{2,0,1:T(8,128)(2,1)}), bf16[32,16,192]{2,0,1:T(8,128)(2,1)S(1)}, u32[]{:S(2)}, u32[]{:S(2)}) async-start(bf16[32,16,192]{2,0,1:T(8,128)(2,1)} %copy.29), calls=%async_computation | async-start | bytes 524288 | tf_op jit(solution)/shard_map/all_to_all | solution.py:124
  14.3 0.8 select_reduce_fusion
  15.2 3.9 %fusion = bf16[3072,3072]{1,0:T(8,128)(2,1)S(1)} fusion(s32[3072]{0:T(1024)S(1)} %eq.57, s32[16,3072]{1,0:T(8,128)S(1)} %select_reduce_fusion), kind=kLoop, calls=%fused_computation.1 | loop fusion | flops 18874368 | bytes 19083264 | tf_op jit(solution)/shard_map/layer_one_mean/convert_element_type | solution.py:111
  19.1 2.8 %collective-permute-start.3 = (bf16[2,192,256]{2,1,0:T(8,128)(2,1)S(1)}, bf16[2,192,256]{2,1,0:T(8,128)(2,1)S(1)}, u32[]{:S(2)}, u32[]{:S(2)}) collective-permute-start(bf16[2,192,256]{2,1,0:T(8,128)(2,1)S(1)} %get-tuple-element.16), channel_id=1, source_target_pairs={{0,8},{1,9},{2,10},{3,11},{4,12},{5,13},{6,14},{7,15},{8,0},{9,1},... | collective-permute-start | bytes 589832 | tf_op jit(solution)/shard_map/layer_one_mean/ppermute | solution.py:29
  22.0 1.5 %collective-permute-start.2 = (bf16[2,192,256]{2,1,0:T(8,128)(2,1)S(1)}, bf16[2,192,256]{2,1,0:T(8,128)(2,1)S(1)}, u32[]{:S(2)}, u32[]{:S(2)}) collective-permute-start(bf16[2,192,256]{2,1,0:T(8,128)(2,1)S(1)} %get-tuple-element.15), channel_id=1, source_target_pairs={{0,4},{1,5},{2,6},{3,7},{4,0},{5,1},{6,2},{7,3},{8,12},{9,13},{10,... | collective-permute-start | bytes 589832 | tf_op jit(solution)/shard_map/layer_one_mean/ppermute | solution.py:29
  23.4 3.4 %fusion.2 = bf16[32,3072]{1,0:T(8,128)(2,1)S(1)} fusion(bf16[32,3072]{1,0:T(8,128)(2,1)S(1)} %copy-done.3, bf16[3072,3072]{1,0:T(8,128)(2,1)S(1)} %fusion, f32[3072]{0:T(1024)S(1)} %convert_divide_fusion), kind=kOutput, calls=%fused_computation.5 | convolution fusion | flops 604176384 | bytes 19279872 | tf_op jit(solution)/shard_map/layer_one_mean/dot_general | solution.py:22
  26.8 5.5 %collective-permute-done.3 = bf16[2,192,256]{2,1,0:T(8,128)(2,1)S(1)} collective-permute-done((bf16[2,192,256]{2,1,0:T(8,128)(2,1)S(1)}, bf16[2,192,256]{2,1,0:T(8,128)(2,1)S(1)}, u32[]{:S(2)}, u32[]{:S(2)}) %collective-permute-start.3) | collective-permute-done | bytes 196640 | tf_op jit(solution)/shard_map/layer_one_mean/ppermute | solution.py:29
  32.5 0.9 collective-permute-start.5
  33.4 1.5 %collective-permute-start.4 = (bf16[2,2,192,256]{3,2,0,1:T(8,128)(2,1)S(1)}, bf16[2,2,192,256]{3,2,0,1:T(8,128)(2,1)S(1)}, u32[]{:S(2)}, u32[]{:S(2)}) collective-permute-start(bf16[2,2,192,256]{3,2,0,1:T(8,128)(2,1)S(1)} %pad_maximum_fusion.9), channel_id=1, source_target_pairs={{0,2},{1,3},{2,0},{3,1},{4,6},{5,7},{6,4},{7,5},{8,10},{9,11},{10,... | collective-permute-start | bytes 1179656 | tf_op jit(solution)/shard_map/ppermute | solution.py:29
  34.8 0.3 all_to_all.32
  35.1 0.8 copy.30
  35.9 3.8 %all-to-all-start.1 = ((bf16[32,16,192]{2,0,1:T(8,128)(2,1)}), bf16[32,16,192]{2,0,1:T(8,128)(2,1)S(1)}, u32[]{:S(2)}, u32[]{:S(2)}) async-start(bf16[32,16,192]{2,0,1:T(8,128)(2,1)} %copy.30), calls=%async_computation.1 | async-start | bytes 524288 | tf_op jit(solution)/shard_map/all_to_all | solution.py:125
  39.7 2.1 %fusion.24 = f32[192,512]{1,0:T(8,128)} fusion(bf16[512,192]{1,0:T(8,128)(2,1)S(1)} %bitcast.148, bf16[1024,512]{1,0:T(8,128)(2,1)} %param.8), kind=kOutput, calls=%fused_computation.56 | convolution fusion | flops 100663296 | bytes 1114112 | tf_op jit(solution)/shard_map/dot_general | solution.py:22
  41.8 1.6 %collective-permute-done.5 = bf16[2,2,192,256]{3,2,1,0:T(8,128)(2,1)S(1)} collective-permute-done((bf16[2,2,192,256]{3,2,1,0:T(8,128)(2,1)S(1)}, bf16[2,2,192,256]{3,2,1,0:T(8,128)(2,1)S(1)}, u32[]{:S(2)}, u32[]{:S(2)}) %collective-permute-start.5) | collective-permute-done | bytes 393248 | tf_op jit(solution)/shard_map/ppermute | solution.py:29
  43.9 5.8 %all-to-all-done.1 = bf16[32,16,192]{2,0,1:T(8,128)(2,1)S(1)} async-done(((bf16[32,16,192]{2,0,1:T(8,128)(2,1)}), bf16[32,16,192]{2,0,1:T(8,128)(2,1)S(1)}, u32[]{:S(2)}, u32[]{:S(2)}) %all-to-all-start.1) | async-done | bytes 196640 | tf_op jit(solution)/shard_map/all_to_all | solution.py:125
  49.7 2.1 %multiply_convert_fusion = (bf16[192,512]{1,0:T(8,128)(2,1)S(1)}, f32[192,512]{1,0:T(8,128)}) fusion(f32[192,512]{1,0:T(8,128)S(1)} %copy-done.9, bf16[512,192]{1,0:T(8,128)(2,1)S(1)} %bitcast.154, bf16[1024,512]{1,0:T(8,128)(2,1)} %param.8), kind=kOutput, calls=%fused_computation.71 | convolution fusion | flops 101253120 | bytes 1703936 | tf_op jit(solution)/shard_map/dot_general | solution.py:22
  51.8 1.1 collective-permute-start.6
  53.0 1.4 %bitcast_compare_fusion.1 = pred[3072,192]{1,0:T(32,128)(4,1)} fusion(s32[3072]{0:T(1024)S(1)} %eq.57, s32[16,192]{1,0:T(8,128)S(1)} %constant_dynamic-slice_fusion.3), kind=kLoop, calls=%fused_computation.14 | loop fusion | flops 589824 | bytes 614400 | tf_op jit(solution)/shard_map/neighbor_tables/eq | solution.py:131
  54.4 5.0 %collective-permute-done.6 = bf16[192,256]{1,0:T(8,128)(2,1)S(1)} collective-permute-done((bf16[192,256]{1,0:T(8,128)(2,1)S(1)}, bf16[192,256]{1,0:T(8,128)(2,1)S(1)}, u32[]{:S(2)}, u32[]{:S(2)}) %collective-permute-start.6) | collective-permute-done | bytes 98336 | tf_op jit(solution)/shard_map/ppermute | solution.py:29
  59.7 2.1 %collective-permute-start.11 = (bf16[2,192,256]{2,1,0:T(8,128)(2,1)S(1)}, bf16[2,192,256]{2,1,0:T(8,128)(2,1)S(1)}, u32[]{:S(2)}, u32[]{:S(2)}) collective-permute-start(bf16[2,192,256]{2,1,0:T(8,128)(2,1)S(1)} %pad_maximum_fusion.16), channel_id=1, source_target_pairs={{0,8},{1,9},{2,10},{3,11},{4,12},{5,13},{6,14},{7,15},{8,0},{9,1},... | collective-permute-start | bytes 589832 | tf_op jit(solution)/shard_map/ppermute | solution.py:29
  61.9 6.8 %collective-permute-done.8 = bf16[2,192,256]{2,1,0:T(8,128)(2,1)S(1)} collective-permute-done((bf16[2,192,256]{2,1,0:T(8,128)(2,1)S(1)}, bf16[2,192,256]{2,1,0:T(8,128)(2,1)S(1)}, u32[]{:S(2)}, u32[]{:S(2)}) %collective-permute-start.8) | collective-permute-done | bytes 196640 | tf_op jit(solution)/shard_map/ppermute | solution.py:29
  68.8 1.2 collective-permute-start.9
  69.9 2.3 %collective-permute-done.11 = bf16[2,192,256]{2,1,0:T(8,128)(2,1)S(1)} collective-permute-done((bf16[2,192,256]{2,1,0:T(8,128)(2,1)S(1)}, bf16[2,192,256]{2,1,0:T(8,128)(2,1)S(1)}, u32[]{:S(2)}, u32[]{:S(2)}) %collective-permute-start.11) | collective-permute-done | bytes 196640 | tf_op jit(solution)/shard_map/ppermute | solution.py:29
  72.4 0.3 fusion.37
  72.8 5.9 %collective-permute-done.9 = bf16[2,2,192,256]{3,2,0,1:T(8,128)(2,1)S(1)} collective-permute-done((bf16[2,2,192,256]{3,2,0,1:T(8,128)(2,1)S(1)}, bf16[2,2,192,256]{3,2,0,1:T(8,128)(2,1)S(1)}, u32[]{:S(2)}, u32[]{:S(2)}) %collective-permute-start.9) | collective-permute-done | bytes 393248 | tf_op jit(solution)/shard_map/ppermute | solution.py:29
  78.9 4.1 %collective-permute-done.12 = bf16[2,2,192,256]{3,2,1,0:T(8,128)(2,1)S(1)} collective-permute-done((bf16[2,2,192,256]{3,2,1,0:T(8,128)(2,1)S(1)}, bf16[2,2,192,256]{3,2,1,0:T(8,128)(2,1)S(1)}, u32[]{:S(2)}, u32[]{:S(2)}) %collective-permute-start.12) | collective-permute-done | bytes 393248 | tf_op jit(solution)/shard_map/ppermute | solution.py:29
  84.1 1.6 %fusion.7 = f32[192,512]{1,0:T(8,128)S(1)} fusion(bf16[3072,256]{1,0:T(8,128)(2,1)S(1)} %bitcast.153, bf16[3072,256]{1,0:T(8,128)(2,1)S(1)} %bitcast.151, s32[3072]{0:T(1024)S(1)} %bitcast.156), kind=kOutput, calls=%fused_computation.10 | convolution fusion | flops 610861056 | bytes 3551232 | tf_op jit(solution)/shard_map/dot_general | solution.py:22
  85.7 0.4 fusion.20
  86.1 0.3 convolution_bitcast_fusion
  86.4 0.3 fusion.36
  87.5 1.0 copy-done.6
  88.5 1.1 fusion.17
  89.6 0.3 fusion.38
  90.0 0.4 pad_maximum_fusion
  90.4 0.3 fusion.33
  90.8 1.4 %copy-done.1 = f32[2048,256]{1,0:T(8,128)} copy-done((f32[2048,256]{1,0:T(8,128)}, f32[2048,256]{1,0:T(8,128)S(1)}, u32[]{:S(2)}) %copy-start.1) | copy-done | bytes 2097176
  92.1 1.1 dynamic-slice_bitcast_fusion
  93.2 0.5 collective-permute-start.16
  93.9 1.0 copy.43
  95.0 1.3 fusion.27
  96.3 1.4 %bitcast_add_fusion.1 = f32[2,2,2,2,64,256]{5,4,3,2,1,0:T(8,128)S(1)} fusion(f32[2,2,2,2,64,256]{5,4,3,2,1,0:T(8,128)} %collective-permute-done.16, f32[2,2,2,2,2,64,256]{6,5,4,3,2,1,0:T(8,128)S(1)} %bitcast.147, s32[]{:T(128)S(6)} %select_n.252), kind=kLoop, calls=%fused_computation.36 | loop fusion | flops 262144 | bytes 3145732 | tf_op jit(solution)/shard_map/weight_grad_sum/add | solution.py:45
  97.8 1.6 %collective-permute-start.17 = (f32[2,2,2,64,256]{4,3,2,1,0:T(8,128)S(1)}, f32[2,2,2,64,256]{4,3,2,1,0:T(8,128)S(1)}, u32[]{:S(2)}, u32[]{:S(2)}) collective-permute-start(f32[2,2,2,64,256]{4,3,2,1,0:T(8,128)S(1)} %dynamic-slice_bitcast_fusion.2), channel_id=1, source_target_pairs={{0,16},{16,0},{1,17},{17,1},{2,18},{18,2},{3,19},{19,3},{4,20},{20... | collective-permute-start | bytes 1572872 | tf_op jit(solution)/shard_map/weight_grad_sum/ppermute | solution.py:29
  99.3 1.5 %bitcast_add_fusion = f32[2,2,2,2,64,256]{5,4,2,1,0,3:T(8,128)S(1)} fusion(f32[2,2,2,2,64,256]{5,4,2,1,0,3:T(8,128)} %collective-permute-done.21, f32[2,2,2,2,1,64,256]{6,5,4,3,2,1,0:T(8,128)S(1)} %get-tuple-element.30), kind=kLoop, calls=%fused_computation.35 | loop fusion | flops 262144 | bytes 3145728 | tf_op jit(solution)/shard_map/weight_grad_sum/add | solution.py:45
  100.8 0.3 collective-permute-start.22
  101.2 1.0 fusion.22
  102.1 9.9 %collective-permute-done.17 = f32[2,2,2,64,256]{4,3,2,1,0:T(8,128)S(1)} collective-permute-done((f32[2,2,2,64,256]{4,3,2,1,0:T(8,128)S(1)}, f32[2,2,2,64,256]{4,3,2,1,0:T(8,128)S(1)}, u32[]{:S(2)}, u32[]{:S(2)}) %collective-permute-start.17) | collective-permute-done | bytes 524320 | tf_op jit(solution)/shard_map/weight_grad_sum/ppermute | solution.py:29
  112.2 0.3 collective-permute-start.18
  112.5 2.7 %collective-permute-done.22 = f32[2,2,2,64,256]{4,3,2,1,0:T(8,128)S(1)} collective-permute-done((f32[2,2,2,64,256]{4,3,2,1,0:T(8,128)S(1)}, f32[2,2,2,64,256]{4,3,2,1,0:T(8,128)S(1)}, u32[]{:S(2)}, u32[]{:S(2)}) %collective-permute-start.22) | collective-permute-done | bytes 524320 | tf_op jit(solution)/shard_map/weight_grad_sum/ppermute | solution.py:29
  115.6 4.9 %collective-permute-done.18 = f32[2,2,64,256]{3,2,1,0:T(8,128)S(1)} collective-permute-done((f32[2,2,64,256]{3,2,1,0:T(8,128)S(1)}, f32[2,2,64,256]{3,2,1,0:T(8,128)S(1)}, u32[]{:S(2)}, u32[]{:S(2)}) %collective-permute-start.18) | collective-permute-done | bytes 262176 | tf_op jit(solution)/shard_map/weight_grad_sum/ppermute | solution.py:29
  120.6 0.7 collective-permute-start.19
  121.3 1.3 collective-permute-done.23
  122.7 0.5 collective-permute-start.24
  123.2 5.5 %collective-permute-done.19 = f32[2,64,256]{2,1,0:T(8,128)S(1)} collective-permute-done((f32[2,64,256]{2,1,0:T(8,128)S(1)}, f32[2,64,256]{2,1,0:T(8,128)S(1)}, u32[]{:S(2)}, u32[]{:S(2)}) %collective-permute-start.19) | collective-permute-done | bytes 131104 | tf_op jit(solution)/shard_map/weight_grad_sum/ppermute | solution.py:29
  128.8 0.6 collective-permute-done.24
  129.4 1.9 %collective-permute-start.25 = (f32[64,256]{1,0:T(8,128)S(1)}, f32[64,256]{1,0:T(8,128)S(1)}, u32[]{:S(2)}, u32[]{:S(2)}) collective-permute-start(f32[64,256]{1,0:T(8,128)S(1)} %dynamic-slice_bitcast_fusion.7), channel_id=1, source_target_pairs={{0,8},{1,9},{2,10},{3,11},{4,12},{5,13},{6,14},{7,15},{8,0},{9,1},... | collective-permute-start | bytes 196616 | tf_op jit(solution)/shard_map/weight_grad_sum/ppermute | solution.py:29
  131.2 2.0 %collective-permute-done.20 = f32[64,256]{1,0:T(8,128)S(1)} collective-permute-done((f32[64,256]{1,0:T(8,128)S(1)}, f32[64,256]{1,0:T(8,128)S(1)}, u32[]{:S(2)}, u32[]{:S(2)}) %collective-permute-start.20) | collective-permute-done | bytes 65568 | tf_op jit(solution)/shard_map/weight_grad_sum/ppermute | solution.py:29
  133.3 1.4 %collective-permute-done.25 = f32[64,256]{1,0:T(8,128)S(1)} collective-permute-done((f32[64,256]{1,0:T(8,128)S(1)}, f32[64,256]{1,0:T(8,128)S(1)}, u32[]{:S(2)}, u32[]{:S(2)}) %collective-permute-start.25) | collective-permute-done | bytes 65568 | tf_op jit(solution)/shard_map/weight_grad_sum/ppermute | solution.py:29
  134.6 0.7 pad_maximum_fusion.17
  (106 shorter events, 4.7 us)
Async XLA Ops:
  0.6 0.9 copy-start
  0.6 13.5 %copy-start.12 = (s32[3072]{0:T(1024)S(1)}, s32[3072]{0:T(1024)}, u32[]{:S(2)}) copy-start(s32[3072]{0:T(1024)} %param.12) | copy-start | bytes 36868
  0.7 13.6 %copy-start.11 = (s32[3072,8]{0,1:T(8,128)S(1)}, s32[3072,8]{0,1:T(8,128)}, u32[]{:S(2)}) copy-start(s32[3072,8]{0,1:T(8,128)} %param.10) | copy-start | bytes 294916
  0.7 13.6 %copy-start.10 = (s32[3072,8]{0,1:T(8,128)S(1)}, s32[3072,8]{0,1:T(8,128)}, u32[]{:S(2)}) copy-start(s32[3072,8]{0,1:T(8,128)} %param.11) | copy-start | bytes 294916
  3.0 16.1 %collective-permute-start = (bf16[192,256]{1,0:T(8,128)(2,1)S(1)}, bf16[192,256]{1,0:T(8,128)(2,1)S(1)}, u32[]{:S(2)}, u32[]{:S(2)}) collective-permute-start(bf16[192,256]{1,0:T(8,128)(2,1)S(1)} %get-tuple-element.71), channel_id=1, source_target_pairs={{0,8},{1,9},{2,10},{3,11},{4,12},{5,13},{6,14},{7,15},{8,0},{9,1},... | collective-permute-start | bytes 294920 | tf_op jit(solution)/shard_map/ppermute | solution.py:29
  7.1 12.0 %collective-permute-start.1 = (bf16[192,256]{1,0:T(8,128)(2,1)S(1)}, bf16[192,256]{1,0:T(8,128)(2,1)S(1)}, u32[]{:S(2)}, u32[]{:S(2)}) collective-permute-start(bf16[192,256]{1,0:T(8,128)(2,1)S(1)} %get-tuple-element.70), channel_id=1, source_target_pairs={{0,2},{1,3},{2,0},{3,1},{4,6},{5,7},{6,4},{7,5},{8,10},{9,11},{10,... | collective-permute-start | bytes 294920 | tf_op jit(solution)/shard_map/ppermute | solution.py:29
  10.6 25.3 %all-to-all-start = ((bf16[32,16,192]{2,0,1:T(8,128)(2,1)}), bf16[32,16,192]{2,0,1:T(8,128)(2,1)S(1)}, u32[]{:S(2)}, u32[]{:S(2)}) async-start(bf16[32,16,192]{2,0,1:T(8,128)(2,1)} %copy.29), calls=%async_computation | async-start | bytes 524288 | tf_op jit(solution)/shard_map/all_to_all | solution.py:124
  15.1 8.3 %copy-start.3 = (bf16[32,3072]{1,0:T(8,128)(2,1)S(1)}, bf16[32,3072]{1,0:T(8,128)(2,1)}, u32[]{:S(2)}) copy-start(bf16[32,3072]{1,0:T(8,128)(2,1)} %param.7) | copy-start | bytes 589828
  19.1 13.1 %collective-permute-start.3 = (bf16[2,192,256]{2,1,0:T(8,128)(2,1)S(1)}, bf16[2,192,256]{2,1,0:T(8,128)(2,1)S(1)}, u32[]{:S(2)}, u32[]{:S(2)}) collective-permute-start(bf16[2,192,256]{2,1,0:T(8,128)(2,1)S(1)} %get-tuple-element.16), channel_id=1, source_target_pairs={{0,8},{1,9},{2,10},{3,11},{4,12},{5,13},{6,14},{7,15},{8,0},{9,1},... | collective-permute-start | bytes 589832 | tf_op jit(solution)/shard_map/layer_one_mean/ppermute | solution.py:29
  22.0 10.4 %collective-permute-start.2 = (bf16[2,192,256]{2,1,0:T(8,128)(2,1)S(1)}, bf16[2,192,256]{2,1,0:T(8,128)(2,1)S(1)}, u32[]{:S(2)}, u32[]{:S(2)}) collective-permute-start(bf16[2,192,256]{2,1,0:T(8,128)(2,1)S(1)} %get-tuple-element.15), channel_id=1, source_target_pairs={{0,4},{1,5},{2,6},{3,7},{4,0},{5,1},{6,2},{7,3},{8,12},{9,13},{10,... | collective-permute-start | bytes 589832 | tf_op jit(solution)/shard_map/layer_one_mean/ppermute | solution.py:29
  32.5 10.8 %collective-permute-start.5 = (bf16[2,2,192,256]{3,2,1,0:T(8,128)(2,1)S(1)}, bf16[2,2,192,256]{3,2,1,0:T(8,128)(2,1)S(1)}, u32[]{:S(2)}, u32[]{:S(2)}) collective-permute-start(bf16[2,2,192,256]{3,2,1,0:T(8,128)(2,1)S(1)} %pad_maximum_fusion.10), channel_id=1, source_target_pairs={{0,4},{1,5},{2,6},{3,7},{4,0},{5,1},{6,2},{7,3},{8,12},{9,13},{10,... | collective-permute-start | bytes 1179656 | tf_op jit(solution)/shard_map/ppermute | solution.py:29
  33.4 10.4 %collective-permute-start.4 = (bf16[2,2,192,256]{3,2,0,1:T(8,128)(2,1)S(1)}, bf16[2,2,192,256]{3,2,0,1:T(8,128)(2,1)S(1)}, u32[]{:S(2)}, u32[]{:S(2)}) collective-permute-start(bf16[2,2,192,256]{3,2,0,1:T(8,128)(2,1)S(1)} %pad_maximum_fusion.9), channel_id=1, source_target_pairs={{0,2},{1,3},{2,0},{3,1},{4,6},{5,7},{6,4},{7,5},{8,10},{9,11},{10,... | collective-permute-start | bytes 1179656 | tf_op jit(solution)/shard_map/ppermute | solution.py:29
  35.9 13.8 %all-to-all-start.1 = ((bf16[32,16,192]{2,0,1:T(8,128)(2,1)}), bf16[32,16,192]{2,0,1:T(8,128)(2,1)S(1)}, u32[]{:S(2)}, u32[]{:S(2)}) async-start(bf16[32,16,192]{2,0,1:T(8,128)(2,1)} %copy.30), calls=%async_computation.1 | async-start | bytes 524288 | tf_op jit(solution)/shard_map/all_to_all | solution.py:125
  43.4 6.3 %copy-start.9 = (f32[192,512]{1,0:T(8,128)S(1)}, f32[192,512]{1,0:T(8,128)}, u32[]{:S(2)}) copy-start(f32[192,512]{1,0:T(8,128)} %fusion.24) | copy-start | bytes 1179652
  51.8 7.6 %collective-permute-start.6 = (bf16[192,256]{1,0:T(8,128)(2,1)S(1)}, bf16[192,256]{1,0:T(8,128)(2,1)S(1)}, u32[]{:S(2)}, u32[]{:S(2)}) collective-permute-start(bf16[192,256]{1,0:T(8,128)(2,1)S(1)} %get-tuple-element.67), channel_id=1, source_target_pairs={{0,8},{1,9},{2,10},{3,11},{4,12},{5,13},{6,14},{7,15},{8,0},{9,1},... | collective-permute-start | bytes 294920 | tf_op jit(solution)/shard_map/ppermute | solution.py:29
  53.0 6.5 %collective-permute-start.7 = (bf16[192,256]{1,0:T(8,128)(2,1)S(1)}, bf16[192,256]{1,0:T(8,128)(2,1)S(1)}, u32[]{:S(2)}, u32[]{:S(2)}) collective-permute-start(bf16[192,256]{1,0:T(8,128)(2,1)S(1)} %get-tuple-element.66), channel_id=1, source_target_pairs={{0,2},{1,3},{2,0},{3,1},{4,6},{5,7},{6,4},{7,5},{8,10},{9,11},{10,... | collective-permute-start | bytes 294920 | tf_op jit(solution)/shard_map/ppermute | solution.py:29
  59.6 9.1 %collective-permute-start.8 = (bf16[2,192,256]{2,1,0:T(8,128)(2,1)S(1)}, bf16[2,192,256]{2,1,0:T(8,128)(2,1)S(1)}, u32[]{:S(2)}, u32[]{:S(2)}) collective-permute-start(bf16[2,192,256]{2,1,0:T(8,128)(2,1)S(1)} %pad_maximum_fusion.15), channel_id=1, source_target_pairs={{0,4},{1,5},{2,6},{3,7},{4,0},{5,1},{6,2},{7,3},{8,12},{9,13},{10,... | collective-permute-start | bytes 589832 | tf_op jit(solution)/shard_map/ppermute | solution.py:29
  59.7 23.6 %collective-permute-start.14 = (bf16[2,2,2,192,256]{4,3,0,1,2:T(8,128)(2,1)S(1)}, bf16[2,2,2,192,256]{4,3,0,1,2:T(8,128)(2,1)S(1)}, u32[]{:S(2)}, u32[]{:S(2)}) collective-permute-start(bf16[2,2,2,192,256]{4,3,0,1,2:T(8,128)(2,1)S(1)} %pad_maximum_fusion.5), channel_id=1, source_target_pairs={{0,1},{1,0},{2,3},{3,2},{4,5},{5,4},{6,7},{7,6},{8,9},{9,8},{10,11... | collective-permute-start | bytes 2359304 | tf_op jit(solution)/shard_map/ppermute | solution.py:29
  59.7 12.5 %collective-permute-start.11 = (bf16[2,192,256]{2,1,0:T(8,128)(2,1)S(1)}, bf16[2,192,256]{2,1,0:T(8,128)(2,1)S(1)}, u32[]{:S(2)}, u32[]{:S(2)}) collective-permute-start(bf16[2,192,256]{2,1,0:T(8,128)(2,1)S(1)} %pad_maximum_fusion.16), channel_id=1, source_target_pairs={{0,8},{1,9},{2,10},{3,11},{4,12},{5,13},{6,14},{7,15},{8,0},{9,1},... | collective-permute-start | bytes 589832 | tf_op jit(solution)/shard_map/ppermute | solution.py:29
  68.8 9.9 %collective-permute-start.9 = (bf16[2,2,192,256]{3,2,0,1:T(8,128)(2,1)S(1)}, bf16[2,2,192,256]{3,2,0,1:T(8,128)(2,1)S(1)}, u32[]{:S(2)}, u32[]{:S(2)}) collective-permute-start(bf16[2,2,192,256]{3,2,0,1:T(8,128)(2,1)S(1)} %pad_maximum_fusion.11), channel_id=1, source_target_pairs={{0,2},{1,3},{2,0},{3,1},{4,6},{5,7},{6,4},{7,5},{8,10},{9,11},{10,... | collective-permute-start | bytes 1179656 | tf_op jit(solution)/shard_map/ppermute | solution.py:29
  72.3 10.7 %collective-permute-start.12 = (bf16[2,2,192,256]{3,2,1,0:T(8,128)(2,1)S(1)}, bf16[2,2,192,256]{3,2,1,0:T(8,128)(2,1)S(1)}, u32[]{:S(2)}, u32[]{:S(2)}) collective-permute-start(bf16[2,2,192,256]{3,2,1,0:T(8,128)(2,1)S(1)} %pad_maximum_fusion.12), channel_id=1, source_target_pairs={{0,4},{1,5},{2,6},{3,7},{4,0},{5,1},{6,2},{7,3},{8,12},{9,13},{10,... | collective-permute-start | bytes 1179656 | tf_op jit(solution)/shard_map/ppermute | solution.py:29
  72.7 11.0 %collective-permute-start.15 = (bf16[2,2,2,192,256]{4,3,2,0,1:T(8,128)(2,1)S(1)}, bf16[2,2,2,192,256]{4,3,2,0,1:T(8,128)(2,1)S(1)}, u32[]{:S(2)}, u32[]{:S(2)}) collective-permute-start(bf16[2,2,2,192,256]{4,3,2,0,1:T(8,128)(2,1)S(1)} %pad_maximum_fusion.6), channel_id=1, source_target_pairs={{0,1},{1,0},{2,3},{3,2},{4,5},{5,4},{6,7},{7,6},{8,9},{9,8},{10,11... | collective-permute-start | bytes 2359304 | tf_op jit(solution)/shard_map/ppermute | solution.py:29
  78.8 7.8 %collective-permute-start.10 = (bf16[2,2,2,192,256]{4,3,0,1,2:T(8,128)(2,1)S(1)}, bf16[2,2,2,192,256]{4,3,0,1,2:T(8,128)(2,1)S(1)}, u32[]{:S(2)}, u32[]{:S(2)}) collective-permute-start(bf16[2,2,2,192,256]{4,3,0,1,2:T(8,128)(2,1)S(1)} %pad_maximum_fusion.7), channel_id=1, source_target_pairs={{0,1},{1,0},{2,3},{3,2},{4,5},{5,4},{6,7},{7,6},{8,9},{9,8},{10,11... | collective-permute-start | bytes 2359304 | tf_op jit(solution)/shard_map/ppermute | solution.py:29
  83.2 3.9 %collective-permute-start.13 = (bf16[2,2,2,192,256]{4,3,2,0,1:T(8,128)(2,1)S(1)}, bf16[2,2,2,192,256]{4,3,2,0,1:T(8,128)(2,1)S(1)}, u32[]{:S(2)}, u32[]{:S(2)}) collective-permute-start(bf16[2,2,2,192,256]{4,3,2,0,1:T(8,128)(2,1)S(1)} %pad_maximum_fusion.8), channel_id=1, source_target_pairs={{0,1},{1,0},{2,3},{3,2},{4,5},{5,4},{6,7},{7,6},{8,9},{9,8},{10,11... | collective-permute-start | bytes 2359304 | tf_op jit(solution)/shard_map/ppermute | solution.py:29
  84.1 1.6 %copy-start.4 = (bf16[1024,512]{1,0:T(8,128)(2,1)S(1)}, bf16[1024,512]{1,0:T(8,128)(2,1)}, u32[]{:S(2)}) copy-start(bf16[1024,512]{1,0:T(8,128)(2,1)} %param.9) | copy-start | bytes 3145732
  84.1 1.6 %copy-start.13 = (f32[192,512]{1,0:T(8,128)S(1)}, f32[192,512]{1,0:T(8,128)}, u32[]{:S(2)}) copy-start(f32[192,512]{1,0:T(8,128)} %get-tuple-element.73) | copy-start | bytes 1179652
  87.4 1.1 copy-start.6
  89.6 0.8 copy-start.7
  90.8 1.4 %copy-start.1 = (f32[2048,256]{1,0:T(8,128)}, f32[2048,256]{1,0:T(8,128)S(1)}, u32[]{:S(2)}) copy-start(f32[2048,256]{1,0:T(8,128)S(1)} %get-tuple-element.28) | copy-start | bytes 6291460
  93.2 3.1 %collective-permute-start.16 = (f32[2,2,2,2,64,256]{5,4,3,2,1,0:T(8,128)}, f32[2,2,2,2,64,256]{5,4,3,2,1,0:T(8,128)}, u32[]{:S(2)}, u32[]{:S(2)}) collective-permute-start(f32[2,2,2,2,64,256]{5,4,3,2,1,0:T(8,128)} %dynamic-slice_bitcast_fusion), channel_id=1, source_target_pairs={{0,1},{1,0},{2,3},{3,2},{4,5},{5,4},{6,7},{7,6},{8,9},{9,8},{10,11... | collective-permute-start | bytes 3145736 | tf_op jit(solution)/shard_map/weight_grad_sum/ppermute | solution.py:29
  93.9 2.5 %copy-start.2 = (f32[2048,256]{1,0:T(8,128)S(1)}, f32[2048,256]{1,0:T(8,128)}, u32[]{:S(2)}) copy-start(f32[2048,256]{1,0:T(8,128)} %copy-done.1) | copy-start | bytes 6291460
  94.9 4.4 %collective-permute-start.21 = (f32[2,2,2,2,64,256]{5,4,2,1,0,3:T(8,128)}, f32[2,2,2,2,64,256]{5,4,2,1,0,3:T(8,128)}, u32[]{:S(2)}, u32[]{:S(2)}) collective-permute-start(f32[2,2,2,2,64,256]{5,4,2,1,0,3:T(8,128)} %bitcast.144), channel_id=1, source_target_pairs={{0,1},{1,0},{2,3},{3,2},{4,5},{5,4},{6,7},{7,6},{8,9},{9,8},{10,11... | collective-permute-start | bytes 3145736 | tf_op jit(solution)/shard_map/weight_grad_sum/ppermute | solution.py:29
  97.8 14.3 %collective-permute-start.17 = (f32[2,2,2,64,256]{4,3,2,1,0:T(8,128)S(1)}, f32[2,2,2,64,256]{4,3,2,1,0:T(8,128)S(1)}, u32[]{:S(2)}, u32[]{:S(2)}) collective-permute-start(f32[2,2,2,64,256]{4,3,2,1,0:T(8,128)S(1)} %dynamic-slice_bitcast_fusion.2), channel_id=1, source_target_pairs={{0,16},{16,0},{1,17},{17,1},{2,18},{18,2},{3,19},{19,3},{4,20},{20... | collective-permute-start | bytes 1572872 | tf_op jit(solution)/shard_map/weight_grad_sum/ppermute | solution.py:29
  99.3 1.9 %copy-start.5 = (bf16[1024,512]{1,0:T(8,128)(2,1)S(1)}, bf16[1024,512]{1,0:T(8,128)(2,1)}, u32[]{:S(2)}) copy-start(bf16[1024,512]{1,0:T(8,128)(2,1)} %param.9) | copy-start | bytes 3145732
  99.3 1.9 %copy-start.8 = (bf16[192,512]{1,0:T(8,128)(2,1)S(1)}, bf16[192,512]{1,0:T(8,128)(2,1)}, u32[]{:S(2)}) copy-start(bf16[192,512]{1,0:T(8,128)(2,1)} %copy-done.7) | copy-start | bytes 589828
  100.8 14.4 %collective-permute-start.22 = (f32[2,2,2,64,256]{4,3,2,1,0:T(8,128)S(1)}, f32[2,2,2,64,256]{4,3,2,1,0:T(8,128)S(1)}, u32[]{:S(2)}, u32[]{:S(2)}) collective-permute-start(f32[2,2,2,64,256]{4,3,2,1,0:T(8,128)S(1)} %dynamic-slice_bitcast_fusion.1), channel_id=1, source_target_pairs={{0,2},{1,3},{2,0},{3,1},{4,6},{5,7},{6,4},{7,5},{8,10},{9,11},{10,... | collective-permute-start | bytes 1572872 | tf_op jit(solution)/shard_map/weight_grad_sum/ppermute | solution.py:29
  112.2 8.3 %collective-permute-start.18 = (f32[2,2,64,256]{3,2,1,0:T(8,128)S(1)}, f32[2,2,64,256]{3,2,1,0:T(8,128)S(1)}, u32[]{:S(2)}, u32[]{:S(2)}) collective-permute-start(f32[2,2,64,256]{3,2,1,0:T(8,128)S(1)} %dynamic-slice_bitcast_fusion.4), channel_id=1, source_target_pairs={{0,2},{1,3},{2,0},{3,1},{4,6},{5,7},{6,4},{7,5},{8,10},{9,11},{10,... | collective-permute-start | bytes 786440 | tf_op jit(solution)/shard_map/weight_grad_sum/ppermute | solution.py:29
  115.3 7.3 %collective-permute-start.23 = (f32[2,2,64,256]{3,2,1,0:T(8,128)S(1)}, f32[2,2,64,256]{3,2,1,0:T(8,128)S(1)}, u32[]{:S(2)}, u32[]{:S(2)}) collective-permute-start(f32[2,2,64,256]{3,2,1,0:T(8,128)S(1)} %dynamic-slice_bitcast_fusion.3), channel_id=1, source_target_pairs={{0,16},{16,0},{1,17},{17,1},{2,18},{18,2},{3,19},{19,3},{4,20},{20... | collective-permute-start | bytes 786440 | tf_op jit(solution)/shard_map/weight_grad_sum/ppermute | solution.py:29
  120.6 8.1 %collective-permute-start.19 = (f32[2,64,256]{2,1,0:T(8,128)S(1)}, f32[2,64,256]{2,1,0:T(8,128)S(1)}, u32[]{:S(2)}, u32[]{:S(2)}) collective-permute-start(f32[2,64,256]{2,1,0:T(8,128)S(1)} %dynamic-slice_bitcast_fusion.6), channel_id=1, source_target_pairs={{0,8},{1,9},{2,10},{3,11},{4,12},{5,13},{6,14},{7,15},{8,0},{9,1},... | collective-permute-start | bytes 393224 | tf_op jit(solution)/shard_map/weight_grad_sum/ppermute | solution.py:29
  122.7 6.7 %collective-permute-start.24 = (f32[2,64,256]{2,1,0:T(8,128)S(1)}, f32[2,64,256]{2,1,0:T(8,128)S(1)}, u32[]{:S(2)}, u32[]{:S(2)}) collective-permute-start(f32[2,64,256]{2,1,0:T(8,128)S(1)} %dynamic-slice_bitcast_fusion.5), channel_id=1, source_target_pairs={{0,4},{1,5},{2,6},{3,7},{4,0},{5,1},{6,2},{7,3},{8,12},{9,13},{10,... | collective-permute-start | bytes 393224 | tf_op jit(solution)/shard_map/weight_grad_sum/ppermute | solution.py:29
  128.7 4.5 %collective-permute-start.20 = (f32[64,256]{1,0:T(8,128)S(1)}, f32[64,256]{1,0:T(8,128)S(1)}, u32[]{:S(2)}, u32[]{:S(2)}) collective-permute-start(f32[64,256]{1,0:T(8,128)S(1)} %dynamic-slice_bitcast_fusion.8), channel_id=1, source_target_pairs={{0,4},{1,5},{2,6},{3,7},{4,0},{5,1},{6,2},{7,3},{8,12},{9,13},{10,... | collective-permute-start | bytes 196616 | tf_op jit(solution)/shard_map/weight_grad_sum/ppermute | solution.py:29
  129.4 5.2 %collective-permute-start.25 = (f32[64,256]{1,0:T(8,128)S(1)}, f32[64,256]{1,0:T(8,128)S(1)}, u32[]{:S(2)}, u32[]{:S(2)}) collective-permute-start(f32[64,256]{1,0:T(8,128)S(1)} %dynamic-slice_bitcast_fusion.7), channel_id=1, source_target_pairs={{0,8},{1,9},{2,10},{3,11},{4,12},{5,13},{6,14},{7,15},{8,0},{9,1},... | collective-permute-start | bytes 196616 | tf_op jit(solution)/shard_map/weight_grad_sum/ppermute | solution.py:29
where the time goes:
time: 136 us; the launch traced here: 135 us
  waiting for transfers between devices  65.7 us (48%)
  starting transfers between devices  30.6 us (22%)
  matrix products  15.4 us (11%)
  other arithmetic  13.1 us (10%)
  local copies, waits for them, and re-layouts  9.17 us (7%)
  between operations  1.38 us (1%)
    ppermute x26, waiting for transfers between devices, swap(): return lax.ppermute(values, axis, [(j, j ^ mask) for j in range(size)])  59.9 us
    ppermute x26, starting transfers between devices, swap(): return lax.ppermute(values, axis, [(j, j ^ mask) for j in range(size)])  23.3 us
    dot_general x13, matrix products, contract(): lax.dot_general(left, right, (((left_dim,), (right_dim,)), ((), ())), pre...  15.4 us
    all_to_all x1, waiting for transfers between devices, shards(): lax.all_to_all(agg_one_cols, 'mp', split_axis=1, concat_axis=0, tiled=True)  5.82 us
    convert_element_type x1, other arithmetic, shards(): adjacency = (rowsel[:, None, :] == row_ids).astype(jnp.bfloat16)  3.87 us
    all_to_all x1, starting transfers between devices, shards(): lax.all_to_all(agg_one_cols, 'mp', split_axis=1, concat_axis=0, tiled=True)  3.77 us
    all_to_all x1, starting transfers between devices, shards(): lax.all_to_all(node_features, 'mp', split_axis=1, concat_axis=0, tiled=True)  3.53 us
    add x10, other arithmetic, halving_scatter(): values = keep + got  3.09 us
  transfers between devices with their start and end apart: 28, of which 19 were waited for; matrix products, arithmetic and copies ran while one was open for 18% of the time, Pallas kernels for 0%

commit v1 on v0

--- a/solution.py
+++ b/solution.py
@@ -1,7 +1,34 @@
+import functools
 import jax
 import jax.numpy as jnp
 from jax import lax
 from jax.sharding import PartitionSpec as P
+
+
+def feed_ends(array_here, ax_name, pos_dim, d0):
+    extra = lax.psum(1, ax_name)
+    built = lax.axis_index(ax_name)
+    after, block_last = (extra, built)
+    later = list(array_here.shape)
+    mid_arr = array_here.shape[pos_dim] // after
+    later[pos_dim] = mid_arr
+    long_array = later[d0]
+    later[d0] = long_array * after
+    value_now = jnp.zeros(later, array_here.dtype)
+    for dev in range(after):
+        r1 = lax.dynamic_slice_in_dim(
+            array_here, (block_last ^ dev) * mid_arr, mid_arr, axis=pos_dim
+        )
+        if dev:
+            shaped = tuple(((kk, kk ^ dev) for kk in range(after)))
+            r1 = lax.ppermute(r1, ax_name, shaped)
+        value_now = lax.dynamic_update_slice_in_dim(
+            value_now, r1, (block_last ^ dev) * long_array, axis=d0
+        )
+    return value_now
+
+
+get_the_trails = functools.partial(feed_ends, ax_name="mp", pos_dim=1, d0=0)
 
 
 def column_mean(table, indices, live, inverse):
@@ -122,7 +149,7 @@
     parts, steps_done = advance(parts, steps_done)
     own_feats, own_agg_one = (
         lax.all_to_all(node_features, "mp", split_axis=1, concat_axis=0, tiled=True),
-        lax.all_to_all(agg_one_cols, "mp", split_axis=1, concat_axis=0, tiled=True),
+        get_the_trails(agg_one_cols),
     )
     parts, own_agg_one = lax.optimization_barrier((parts, own_agg_one))
     with jax.named_scope("neighbor_tables"):

time: 136 us -> 156 us (1.15)
  starting transfers between devices: 30.6 us -> 53.1 us
  waiting for transfers between devices: 65.7 us -> 54.4 us
  other arithmetic: 13.1 us -> 18.1 us
  matrix products: 15.4 us -> 20 us
    ppermute x0 -> x15, starting transfers between devices: none -> 21.6 us  [feed_ends(): r1 = lax.ppermute(r1, ax_name, shaped)]
    ppermute x26, waiting for transfers between devices: 59.9 us -> 50.9 us  [swap(): return lax.ppermute(values, axis, [(j, j ^ mask) for j in range(size)])]
    all_to_all x1 -> x0, waiting for transfers between devices: 5.82 us -> none  [shards(): lax.all_to_all(agg_one_cols, 'mp', split_axis=1, concat_axis=0, tiled=True)]
    dot_general x13, matrix products: 15.4 us -> 20 us  [contract(): lax.dot_general(left, right, (((left_dim,), (right_dim,)), ((), ())), pre...]
    ppermute x26, starting transfers between devices: 23.3 us -> 27.5 us  [swap(): return lax.ppermute(values, axis, [(j, j ^ mask) for j in range(size)])]
    all_to_all x1 -> x0, starting transfers between devices: 3.77 us -> none  [shards(): lax.all_to_all(agg_one_cols, 'mp', split_axis=1, concat_axis=0, tiled=True)]
    ppermute x0 -> x15, waiting for transfers between devices: none -> 3.45 us  [feed_ends(): r1 = lax.ppermute(r1, ax_name, shaped)]
    convert_element_type x1, other arithmetic: 3.87 us -> 7.25 us  [shards(): adjacency = (rowsel[:, None, :] == row_ids).astype(jnp.bfloat16)]
  transfers between devices with their start and end apart: 28 -> 42, of which waited for: 19 -> 16; matrix products, arithmetic and copies ran while one was open for 18% -> 22% of each run, Pallas kernels for 0% -> 0%
where the time goes in v1:
time: 156 us
  waiting for transfers between devices  54.4 us (35%)
  starting transfers between devices  53.1 us (34%)
  matrix products  20 us (13%)
  other arithmetic  18.1 us (12%)
  local copies, waits for them, and re-layouts  8.43 us (5%)
  between operations  1.6 us (1%)
    ppermute x26, waiting for transfers between devices, swap(): return lax.ppermute(values, axis, [(j, j ^ mask) for j in range(size)])  50.9 us
    ppermute x26, starting transfers between devices, swap(): return lax.ppermute(values, axis, [(j, j ^ mask) for j in range(size)])  27.5 us
    ppermute x15, starting transfers between devices, feed_ends(): r1 = lax.ppermute(r1, ax_name, shaped)  21.6 us
    dot_general x13, matrix products, contract(): lax.dot_general(left, right, (((left_dim,), (right_dim,)), ((), ())), pre...  20 us
    convert_element_type x1, other arithmetic, shards(): adjacency = (rowsel[:, None, :] == row_ids).astype(jnp.bfloat16)  7.25 us
    all_to_all x1, starting transfers between devices, shards(): lax.all_to_all(node_features, 'mp', split_axis=1, concat_axis=0, tiled=True)  4.08 us
    unnamed x22, local copies, waits for them, and re-layouts  3.45 us
    ppermute x15, waiting for transfers between devices, feed_ends(): r1 = lax.ppermute(r1, ax_name, shaped)  3.45 us
  transfers between devices with their start and end apart: 42, of which 16 were waited for; matrix products, arithmetic and copies ran while one was open for 22% of the time, Pallas kernels for 0%

profile of v1, /device:TPU:0, one launch (start us, length us, event | category | flops | bytes accessed | tf_op | source)
XLA Modules:
  0.0 155.6 jit_solution(16105057386942671410)
XLA Ops:
  0.7 0.8 convert_divide_fusion
  1.6 1.4 fusion.21
  3.0 4.1 %collective-permute-start = (bf16[192,256]{1,0:T(8,128)(2,1)S(1)}, bf16[192,256]{1,0:T(8,128)(2,1)S(1)}, u32[]{:S(2)}, u32[]{:S(2)}) collective-permute-start(bf16[192,256]{1,0:T(8,128)(2,1)S(1)} %get-tuple-element.87), channel_id=1, source_target_pairs={{0,8},{1,9},{2,10},{3,11},{4,12},{5,13},{6,14},{7,15},{8,0},{9,1},... | collective-permute-start | bytes 294920 | tf_op jit(solution)/shard_map/ppermute | solution.py:56
  7.1 1.5 collective-permute-start.1
  8.6 0.7 iota_compare_fusion.3
  9.5 1.8 %select_reduce_fusion = s32[16,3072]{1,0:T(8,128)S(1)} fusion(s32[3072,8]{0,1:T(8,128)} %param.11, s32[3072,8]{0,1:T(8,128)} %param.10, pred[3072,8]{0,1:T(8,128)(4,1)S(1)} %iota_compare_fusion.3), kind=kLoop, calls=%fused_computation.21 | loop fusion | flops 1523712 | bytes 417792 | tf_op jit(solution)/shard_map/reduce_max | solution.py:116
  11.3 7.3 %fusion = bf16[3072,3072]{1,0:T(8,128)(2,1)} fusion(s32[3072]{0:T(1024)S(1)} %eq.57, s32[16,3072]{1,0:T(8,128)S(1)} %select_reduce_fusion), kind=kLoop, calls=%fused_computation.1 | loop fusion | flops 18874368 | bytes 19083264 | tf_op jit(solution)/shard_map/layer_one_mean/convert_element_type | solution.py:138
  19.0 1.6 %collective-permute-start.2 = (bf16[2,192,256]{2,1,0:T(8,128)(2,1)S(1)}, bf16[2,192,256]{2,1,0:T(8,128)(2,1)S(1)}, u32[]{:S(2)}, u32[]{:S(2)}) collective-permute-start(bf16[2,192,256]{2,1,0:T(8,128)(2,1)S(1)} %get-tuple-element.15), channel_id=1, source_target_pairs={{0,4},{1,5},{2,6},{3,7},{4,0},{5,1},{6,2},{7,3},{8,12},{9,13},{10,... | collective-permute-start | bytes 589832 | tf_op jit(solution)/shard_map/layer_one_mean/ppermute | solution.py:56
  20.6 9.7 %fusion.2 = bf16[32,3072]{1,0:T(8,128)(2,1)S(1)} fusion(bf16[32,3072]{1,0:T(8,128)(2,1)S(1)} %copy-done.3, bf16[3072,3072]{1,0:T(8,128)(2,1)} %fusion, f32[3072]{0:T(1024)S(1)} %convert_divide_fusion), kind=kOutput, calls=%fused_computation.5 | convolution fusion | flops 604176384 | bytes 19279872 | tf_op jit(solution)/shard_map/layer_one_mean/dot_general | solution.py:49
  31.2 0.8 copy.28
  32.0 4.1 %all-to-all-start = ((bf16[32,16,192]{2,0,1:T(8,128)(2,1)}), bf16[32,16,192]{2,0,1:T(8,128)(2,1)S(1)}, u32[]{:S(2)}, u32[]{:S(2)}) async-start(bf16[32,16,192]{2,0,1:T(8,128)(2,1)} %copy.28), calls=%async_computation | async-start | bytes 524288 | tf_op jit(solution)/shard_map/all_to_all | solution.py:151
  36.2 1.9 %collective-permute-start.7 = (bf16[32,192]{1,0:T(8,128)(2,1)S(1)}, bf16[32,192]{1,0:T(8,128)(2,1)S(1)}, u32[]{:S(2)}, u32[]{:S(2)}) collective-permute-start(bf16[32,192]{1,0:T(8,128)(2,1)S(1)} %get-tuple-element.81), channel_id=1, source_target_pairs={{0,2},{1,3},{2,0},{3,1},{4,6},{5,7},{6,4},{7,5},{8,10},{9,11},{10,... | collective-permute-start | bytes 36872 | tf_op jit(solution)/shard_map/ppermute | solution.py:24
  38.1 1.5 collective-permute-start.9
  39.9 2.6 %collective-permute-start.11 = (bf16[32,192]{1,0:T(8,128)(2,1)S(1)}, bf16[32,192]{1,0:T(8,128)(2,1)S(1)}, u32[]{:S(2)}, u32[]{:S(2)}) collective-permute-start(bf16[32,192]{1,0:T(8,128)(2,1)S(1)} %get-tuple-element.77), channel_id=1, source_target_pairs={{0,6},{1,7},{2,4},{3,5},{4,2},{5,3},{6,0},{7,1},{8,14},{9,15},{10,... | collective-permute-start | bytes 36872 | tf_op jit(solution)/shard_map/ppermute | solution.py:24
  42.5 2.4 %collective-permute-start.13 = (bf16[32,192]{1,0:T(8,128)(2,1)S(1)}, bf16[32,192]{1,0:T(8,128)(2,1)S(1)}, u32[]{:S(2)}, u32[]{:S(2)}) collective-permute-start(bf16[32,192]{1,0:T(8,128)(2,1)S(1)} %get-tuple-element.75), channel_id=1, source_target_pairs={{0,8},{1,9},{2,10},{3,11},{4,12},{5,13},{6,14},{7,15},{8,0},{9,1},... | collective-permute-start | bytes 36872 | tf_op jit(solution)/shard_map/ppermute | solution.py:24
  45.0 0.6 collective-permute-start.14
  45.6 3.1 %collective-permute-start.15 = (bf16[32,192]{1,0:T(8,128)(2,1)S(1)}, bf16[32,192]{1,0:T(8,128)(2,1)S(1)}, u32[]{:S(2)}, u32[]{:S(2)}) collective-permute-start(bf16[32,192]{1,0:T(8,128)(2,1)S(1)} %get-tuple-element.73), channel_id=1, source_target_pairs={{0,10},{1,11},{2,8},{3,9},{4,14},{5,15},{6,12},{7,13},{8,2},{9,3},... | collective-permute-start | bytes 36872 | tf_op jit(solution)/shard_map/ppermute | solution.py:24
  48.7 1.0 collective-permute-start.16
  49.8 2.3 %collective-permute-start.17 = (bf16[32,192]{1,0:T(8,128)(2,1)S(1)}, bf16[32,192]{1,0:T(8,128)(2,1)S(1)}, u32[]{:S(2)}, u32[]{:S(2)}) collective-permute-start(bf16[32,192]{1,0:T(8,128)(2,1)S(1)} %get-tuple-element.71), channel_id=1, source_target_pairs={{0,12},{1,13},{2,14},{3,15},{4,8},{5,9},{6,10},{7,11},{8,4},{9,5},... | collective-permute-start | bytes 36872 | tf_op jit(solution)/shard_map/ppermute | solution.py:24
  52.0 0.7 collective-permute-start.18
  52.7 4.0 %collective-permute-start.19 = (bf16[32,192]{1,0:T(8,128)(2,1)S(1)}, bf16[32,192]{1,0:T(8,128)(2,1)S(1)}, u32[]{:S(2)}, u32[]{:S(2)}) collective-permute-start(bf16[32,192]{1,0:T(8,128)(2,1)S(1)} %get-tuple-element.69), channel_id=1, source_target_pairs={{0,14},{1,15},{2,12},{3,13},{4,10},{5,11},{6,8},{7,9},{8,6},{9,7},... | collective-permute-start | bytes 36872 | tf_op jit(solution)/shard_map/ppermute | solution.py:24
  56.7 1.0 collective-permute-start.20
  57.8 1.6 %collective-permute-start.4 = (bf16[2,2,192,256]{3,2,0,1:T(8,128)(2,1)S(1)}, bf16[2,2,192,256]{3,2,0,1:T(8,128)(2,1)S(1)}, u32[]{:S(2)}, u32[]{:S(2)}) collective-permute-start(bf16[2,2,192,256]{3,2,0,1:T(8,128)(2,1)S(1)} %pad_maximum_fusion.9), channel_id=1, source_target_pairs={{0,2},{1,3},{2,0},{3,1},{4,6},{5,7},{6,4},{7,5},{8,10},{9,11},{10,... | collective-permute-start | bytes 1179656 | tf_op jit(solution)/shard_map/ppermute | solution.py:56
  59.4 3.4 %collective-permute-done.20 = bf16[32,192]{1,0:T(8,128)(2,1)S(1)} collective-permute-done((bf16[32,192]{1,0:T(8,128)(2,1)S(1)}, bf16[32,192]{1,0:T(8,128)(2,1)S(1)}, u32[]{:S(2)}, u32[]{:S(2)}) %collective-permute-start.20) | collective-permute-done | bytes 12320 | tf_op jit(solution)/shard_map/ppermute | solution.py:24
  62.8 1.3 fusion.24
  64.2 4.8 %collective-permute-done.5 = bf16[2,2,192,256]{3,2,1,0:T(8,128)(2,1)S(1)} collective-permute-done((bf16[2,2,192,256]{3,2,1,0:T(8,128)(2,1)S(1)}, bf16[2,2,192,256]{3,2,1,0:T(8,128)(2,1)S(1)}, u32[]{:S(2)}, u32[]{:S(2)}) %collective-permute-start.5) | collective-permute-done | bytes 393248 | tf_op jit(solution)/shard_map/ppermute | solution.py:56
  69.3 1.0 copy-done.9
  70.2 1.1 multiply_convert_fusion
  71.3 2.0 %collective-permute-start.21 = (bf16[192,256]{1,0:T(8,128)(2,1)S(1)}, bf16[192,256]{1,0:T(8,128)(2,1)S(1)}, u32[]{:S(2)}, u32[]{:S(2)}) collective-permute-start(bf16[192,256]{1,0:T(8,128)(2,1)S(1)} %get-tuple-element.67), channel_id=1, source_target_pairs={{0,8},{1,9},{2,10},{3,11},{4,12},{5,13},{6,14},{7,15},{8,0},{9,1},... | collective-permute-start | bytes 294920 | tf_op jit(solution)/shard_map/ppermute | solution.py:56
  73.3 1.5 collective-permute-start.22
  74.8 1.4 bitcast_compare_fusion.1
  76.2 2.2 %collective-permute-done.21 = bf16[192,256]{1,0:T(8,128)(2,1)S(1)} collective-permute-done((bf16[192,256]{1,0:T(8,128)(2,1)S(1)}, bf16[192,256]{1,0:T(8,128)(2,1)S(1)}, u32[]{:S(2)}, u32[]{:S(2)}) %collective-permute-start.21) | collective-permute-done | bytes 98336 | tf_op jit(solution)/shard_map/ppermute | solution.py:56
  78.5 1.1 collective-permute-start.23
  79.7 3.0 %collective-permute-start.26 = (bf16[2,192,256]{2,1,0:T(8,128)(2,1)S(1)}, bf16[2,192,256]{2,1,0:T(8,128)(2,1)S(1)}, u32[]{:S(2)}, u32[]{:S(2)}) collective-permute-start(bf16[2,192,256]{2,1,0:T(8,128)(2,1)S(1)} %pad_maximum_fusion.16), channel_id=1, source_target_pairs={{0,8},{1,9},{2,10},{3,11},{4,12},{5,13},{6,14},{7,15},{8,0},{9,1},... | collective-permute-start | bytes 589832 | tf_op jit(solution)/shard_map/ppermute | solution.py:56
  82.7 4.5 %collective-permute-done.23 = bf16[2,192,256]{2,1,0:T(8,128)(2,1)S(1)} collective-permute-done((bf16[2,192,256]{2,1,0:T(8,128)(2,1)S(1)}, bf16[2,192,256]{2,1,0:T(8,128)(2,1)S(1)}, u32[]{:S(2)}, u32[]{:S(2)}) %collective-permute-start.23) | collective-permute-done | bytes 196640 | tf_op jit(solution)/shard_map/ppermute | solution.py:56
  87.3 1.5 collective-permute-start.24
  88.8 3.7 %collective-permute-done.26 = bf16[2,192,256]{2,1,0:T(8,128)(2,1)S(1)} collective-permute-done((bf16[2,192,256]{2,1,0:T(8,128)(2,1)S(1)}, bf16[2,192,256]{2,1,0:T(8,128)(2,1)S(1)}, u32[]{:S(2)}, u32[]{:S(2)}) %collective-permute-start.26) | collective-permute-done | bytes 196640 | tf_op jit(solution)/shard_map/ppermute | solution.py:56
  93.0 2.1 %collective-permute-done.24 = bf16[2,2,192,256]{3,2,0,1:T(8,128)(2,1)S(1)} collective-permute-done((bf16[2,2,192,256]{3,2,0,1:T(8,128)(2,1)S(1)}, bf16[2,2,192,256]{3,2,0,1:T(8,128)(2,1)S(1)}, u32[]{:S(2)}, u32[]{:S(2)}) %collective-permute-start.24) | collective-permute-done | bytes 393248 | tf_op jit(solution)/shard_map/ppermute | solution.py:56
  95.4 8.1 %collective-permute-done.27 = bf16[2,2,192,256]{3,2,1,0:T(8,128)(2,1)S(1)} collective-permute-done((bf16[2,2,192,256]{3,2,1,0:T(8,128)(2,1)S(1)}, bf16[2,2,192,256]{3,2,1,0:T(8,128)(2,1)S(1)}, u32[]{:S(2)}, u32[]{:S(2)}) %collective-permute-start.27) | collective-permute-done | bytes 393248 | tf_op jit(solution)/shard_map/ppermute | solution.py:56
  104.5 1.6 %fusion.7 = f32[192,512]{1,0:T(8,128)S(1)} fusion(bf16[3072,256]{1,0:T(8,128)(2,1)S(1)} %bitcast.150, bf16[3072,256]{1,0:T(8,128)(2,1)S(1)} %bitcast.148, s32[3072]{0:T(1024)S(1)} %bitcast.151), kind=kOutput, calls=%fused_computation.10 | convolution fusion | flops 610861056 | bytes 3551232 | tf_op jit(solution)/shard_map/dot_general | solution.py:49
  107.9 1.0 copy-done.6
  108.9 1.1 fusion.17
  111.1 1.3 copy-done.1
  112.5 1.1 dynamic-slice_bitcast_fusion
  114.2 1.1 copy.41
  115.3 1.3 fusion.27
  116.7 1.4 bitcast_add_fusion.1
  118.1 1.6 collective-permute-start.32
  119.7 1.5 bitcast_add_fusion
  121.2 1.6 %collective-permute-start.37 = (f32[2,2,2,64,256]{4,3,2,1,0:T(8,128)S(1)}, f32[2,2,2,64,256]{4,3,2,1,0:T(8,128)S(1)}, u32[]{:S(2)}, u32[]{:S(2)}) collective-permute-start(f32[2,2,2,64,256]{4,3,2,1,0:T(8,128)S(1)} %dynamic-slice_bitcast_fusion.1), channel_id=1, source_target_pairs={{0,2},{1,3},{2,0},{3,1},{4,6},{5,7},{6,4},{7,5},{8,10},{9,11},{10,... | collective-permute-start | bytes 1572872 | tf_op jit(solution)/shard_map/weight_grad_sum/ppermute | solution.py:56
  122.8 1.0 fusion.22
  123.7 8.7 %collective-permute-done.32 = f32[2,2,2,64,256]{4,3,2,1,0:T(8,128)S(1)} collective-permute-done((f32[2,2,2,64,256]{4,3,2,1,0:T(8,128)S(1)}, f32[2,2,2,64,256]{4,3,2,1,0:T(8,128)S(1)}, u32[]{:S(2)}, u32[]{:S(2)}) %collective-permute-start.32) | collective-permute-done | bytes 524320 | tf_op jit(solution)/shard_map/weight_grad_sum/ppermute | solution.py:56
  132.5 1.6 %collective-permute-start.33 = (f32[2,2,64,256]{3,2,1,0:T(8,128)S(1)}, f32[2,2,64,256]{3,2,1,0:T(8,128)S(1)}, u32[]{:S(2)}, u32[]{:S(2)}) collective-permute-start(f32[2,2,64,256]{3,2,1,0:T(8,128)S(1)} %dynamic-slice_bitcast_fusion.4), channel_id=1, source_target_pairs={{0,2},{1,3},{2,0},{3,1},{4,6},{5,7},{6,4},{7,5},{8,10},{9,11},{10,... | collective-permute-start | bytes 786440 | tf_op jit(solution)/shard_map/weight_grad_sum/ppermute | solution.py:56
  134.1 1.4 collective-permute-done.37
  135.9 4.9 %collective-permute-done.33 = f32[2,2,64,256]{3,2,1,0:T(8,128)S(1)} collective-permute-done((f32[2,2,64,256]{3,2,1,0:T(8,128)S(1)}, f32[2,2,64,256]{3,2,1,0:T(8,128)S(1)}, u32[]{:S(2)}, u32[]{:S(2)}) %collective-permute-start.33) | collective-permute-done | bytes 262176 | tf_op jit(solution)/shard_map/weight_grad_sum/ppermute | solution.py:56
  140.9 0.8 collective-permute-start.34
  141.7 1.2 collective-permute-done.38
  143.0 0.6 collective-permute-start.39
  143.6 5.4 %collective-permute-done.34 = f32[2,64,256]{2,1,0:T(8,128)S(1)} collective-permute-done((f32[2,64,256]{2,1,0:T(8,128)S(1)}, f32[2,64,256]{2,1,0:T(8,128)S(1)}, u32[]{:S(2)}, u32[]{:S(2)}) %collective-permute-start.34) | collective-permute-done | bytes 131104 | tf_op jit(solution)/shard_map/weight_grad_sum/ppermute | solution.py:56
  149.1 0.6 collective-permute-done.39
  149.7 2.0 %collective-permute-start.40 = (f32[64,256]{1,0:T(8,128)S(1)}, f32[64,256]{1,0:T(8,128)S(1)}, u32[]{:S(2)}, u32[]{:S(2)}) collective-permute-start(f32[64,256]{1,0:T(8,128)S(1)} %dynamic-slice_bitcast_fusion.7), channel_id=1, source_target_pairs={{0,8},{1,9},{2,10},{3,11},{4,12},{5,13},{6,14},{7,15},{8,0},{9,1},... | collective-permute-start | bytes 196616 | tf_op jit(solution)/shard_map/weight_grad_sum/ppermute | solution.py:56
  151.7 1.8 %collective-permute-done.35 = f32[64,256]{1,0:T(8,128)S(1)} collective-permute-done((f32[64,256]{1,0:T(8,128)S(1)}, f32[64,256]{1,0:T(8,128)S(1)}, u32[]{:S(2)}, u32[]{:S(2)}) %collective-permute-start.35) | collective-permute-done | bytes 65568 | tf_op jit(solution)/shard_map/weight_grad_sum/ppermute | solution.py:56
  153.6 1.4 collective-permute-done.40
  155.0 0.7 pad_maximum_fusion.17
  (143 shorter events, 8.6 us)
Async XLA Ops:
  0.6 0.9 copy-start
  3.0 15.6 %collective-permute-start = (bf16[192,256]{1,0:T(8,128)(2,1)S(1)}, bf16[192,256]{1,0:T(8,128)(2,1)S(1)}, u32[]{:S(2)}, u32[]{:S(2)}) collective-permute-start(bf16[192,256]{1,0:T(8,128)(2,1)S(1)} %get-tuple-element.87), channel_id=1, source_target_pairs={{0,8},{1,9},{2,10},{3,11},{4,12},{5,13},{6,14},{7,15},{8,0},{9,1},... | collective-permute-start | bytes 294920 | tf_op jit(solution)/shard_map/ppermute | solution.py:56
  7.1 11.5 %collective-permute-start.1 = (bf16[192,256]{1,0:T(8,128)(2,1)S(1)}, bf16[192,256]{1,0:T(8,128)(2,1)S(1)}, u32[]{:S(2)}, u32[]{:S(2)}) collective-permute-start(bf16[192,256]{1,0:T(8,128)(2,1)S(1)} %get-tuple-element.86), channel_id=1, source_target_pairs={{0,2},{1,3},{2,0},{3,1},{4,6},{5,7},{6,4},{7,5},{8,10},{9,11},{10,... | collective-permute-start | bytes 294920 | tf_op jit(solution)/shard_map/ppermute | solution.py:56
  11.3 9.3 %copy-start.3 = (bf16[32,3072]{1,0:T(8,128)(2,1)S(1)}, bf16[32,3072]{1,0:T(8,128)(2,1)}, u32[]{:S(2)}) copy-start(bf16[32,3072]{1,0:T(8,128)(2,1)} %param.7) | copy-start | bytes 589828
  18.6 11.7 %collective-permute-start.3 = (bf16[2,192,256]{2,1,0:T(8,128)(2,1)S(1)}, bf16[2,192,256]{2,1,0:T(8,128)(2,1)S(1)}, u32[]{:S(2)}, u32[]{:S(2)}) collective-permute-start(bf16[2,192,256]{2,1,0:T(8,128)(2,1)S(1)} %get-tuple-element.16), channel_id=1, source_target_pairs={{0,8},{1,9},{2,10},{3,11},{4,12},{5,13},{6,14},{7,15},{8,0},{9,1},... | collective-permute-start | bytes 589832 | tf_op jit(solution)/shard_map/layer_one_mean/ppermute | solution.py:56
  19.0 11.4 %collective-permute-start.2 = (bf16[2,192,256]{2,1,0:T(8,128)(2,1)S(1)}, bf16[2,192,256]{2,1,0:T(8,128)(2,1)S(1)}, u32[]{:S(2)}, u32[]{:S(2)}) collective-permute-start(bf16[2,192,256]{2,1,0:T(8,128)(2,1)S(1)} %get-tuple-element.15), channel_id=1, source_target_pairs={{0,4},{1,5},{2,6},{3,7},{4,0},{5,1},{6,2},{7,3},{8,12},{9,13},{10,... | collective-permute-start | bytes 589832 | tf_op jit(solution)/shard_map/layer_one_mean/ppermute | solution.py:56
  30.8 9.0 %collective-permute-start.6 = (bf16[32,192]{1,0:T(8,128)(2,1)S(1)}, bf16[32,192]{1,0:T(8,128)(2,1)S(1)}, u32[]{:S(2)}, u32[]{:S(2)}) collective-permute-start(bf16[32,192]{1,0:T(8,128)(2,1)S(1)} %get-tuple-element.82), channel_id=1, source_target_pairs={{0,1},{1,0},{2,3},{3,2},{4,5},{5,4},{6,7},{7,6},{8,9},{9,8},{10,11... | collective-permute-start | bytes 36872 | tf_op jit(solution)/shard_map/ppermute | solution.py:24
  32.0 30.8 %all-to-all-start = ((bf16[32,16,192]{2,0,1:T(8,128)(2,1)}), bf16[32,16,192]{2,0,1:T(8,128)(2,1)S(1)}, u32[]{:S(2)}, u32[]{:S(2)}) async-start(bf16[32,16,192]{2,0,1:T(8,128)(2,1)} %copy.28), calls=%async_computation | async-start | bytes 524288 | tf_op jit(solution)/shard_map/all_to_all | solution.py:151
  36.2 6.3 %collective-permute-start.7 = (bf16[32,192]{1,0:T(8,128)(2,1)S(1)}, bf16[32,192]{1,0:T(8,128)(2,1)S(1)}, u32[]{:S(2)}, u32[]{:S(2)}) collective-permute-start(bf16[32,192]{1,0:T(8,128)(2,1)S(1)} %get-tuple-element.81), channel_id=1, source_target_pairs={{0,2},{1,3},{2,0},{3,1},{4,6},{5,7},{6,4},{7,5},{8,10},{9,11},{10,... | collective-permute-start | bytes 36872 | tf_op jit(solution)/shard_map/ppermute | solution.py:24
  38.1 4.4 %collective-permute-start.8 = (bf16[32,192]{1,0:T(8,128)(2,1)S(1)}, bf16[32,192]{1,0:T(8,128)(2,1)S(1)}, u32[]{:S(2)}, u32[]{:S(2)}) collective-permute-start(bf16[32,192]{1,0:T(8,128)(2,1)S(1)} %get-tuple-element.80), channel_id=1, source_target_pairs={{0,3},{1,2},{2,1},{3,0},{4,7},{5,6},{6,5},{7,4},{8,11},{9,10},{10,... | collective-permute-start | bytes 36872 | tf_op jit(solution)/shard_map/ppermute | solution.py:24
  38.1 6.9 %collective-permute-start.9 = (bf16[32,192]{1,0:T(8,128)(2,1)S(1)}, bf16[32,192]{1,0:T(8,128)(2,1)S(1)}, u32[]{:S(2)}, u32[]{:S(2)}) collective-permute-start(bf16[32,192]{1,0:T(8,128)(2,1)S(1)} %get-tuple-element.79), channel_id=1, source_target_pairs={{0,4},{1,5},{2,6},{3,7},{4,0},{5,1},{6,2},{7,3},{8,12},{9,13},{10,... | collective-permute-start | bytes 36872 | tf_op jit(solution)/shard_map/ppermute | solution.py:24
  39.6 6.0 %collective-permute-start.10 = (bf16[32,192]{1,0:T(8,128)(2,1)S(1)}, bf16[32,192]{1,0:T(8,128)(2,1)S(1)}, u32[]{:S(2)}, u32[]{:S(2)}) collective-permute-start(bf16[32,192]{1,0:T(8,128)(2,1)S(1)} %get-tuple-element.78), channel_id=1, source_target_pairs={{0,5},{1,4},{2,7},{3,6},{4,1},{5,0},{6,3},{7,2},{8,13},{9,12},{10,... | collective-permute-start | bytes 36872 | tf_op jit(solution)/shard_map/ppermute | solution.py:24
  39.9 8.9 %collective-permute-start.11 = (bf16[32,192]{1,0:T(8,128)(2,1)S(1)}, bf16[32,192]{1,0:T(8,128)(2,1)S(1)}, u32[]{:S(2)}, u32[]{:S(2)}) collective-permute-start(bf16[32,192]{1,0:T(8,128)(2,1)S(1)} %get-tuple-element.77), channel_id=1, source_target_pairs={{0,6},{1,7},{2,4},{3,5},{4,2},{5,3},{6,0},{7,1},{8,14},{9,15},{10,... | collective-permute-start | bytes 36872 | tf_op jit(solution)/shard_map/ppermute | solution.py:24
  42.5 7.3 %collective-permute-start.12 = (bf16[32,192]{1,0:T(8,128)(2,1)S(1)}, bf16[32,192]{1,0:T(8,128)(2,1)S(1)}, u32[]{:S(2)}, u32[]{:S(2)}) collective-permute-start(bf16[32,192]{1,0:T(8,128)(2,1)S(1)} %get-tuple-element.76), channel_id=1, source_target_pairs={{0,7},{1,6},{2,5},{3,4},{4,3},{5,2},{6,1},{7,0},{8,15},{9,14},{10,... | collective-permute-start | bytes 36872 | tf_op jit(solution)/shard_map/ppermute | solution.py:24
  42.5 9.5 %collective-permute-start.13 = (bf16[32,192]{1,0:T(8,128)(2,1)S(1)}, bf16[32,192]{1,0:T(8,128)(2,1)S(1)}, u32[]{:S(2)}, u32[]{:S(2)}) collective-permute-start(bf16[32,192]{1,0:T(8,128)(2,1)S(1)} %get-tuple-element.75), channel_id=1, source_target_pairs={{0,8},{1,9},{2,10},{3,11},{4,12},{5,13},{6,14},{7,15},{8,0},{9,1},... | collective-permute-start | bytes 36872 | tf_op jit(solution)/shard_map/ppermute | solution.py:24
  45.0 7.8 %collective-permute-start.14 = (bf16[32,192]{1,0:T(8,128)(2,1)S(1)}, bf16[32,192]{1,0:T(8,128)(2,1)S(1)}, u32[]{:S(2)}, u32[]{:S(2)}) collective-permute-start(bf16[32,192]{1,0:T(8,128)(2,1)S(1)} %get-tuple-element.74), channel_id=1, source_target_pairs={{0,9},{1,8},{2,11},{3,10},{4,13},{5,12},{6,15},{7,14},{8,1},{9,0},... | collective-permute-start | bytes 36872 | tf_op jit(solution)/shard_map/ppermute | solution.py:24
  45.6 11.1 %collective-permute-start.15 = (bf16[32,192]{1,0:T(8,128)(2,1)S(1)}, bf16[32,192]{1,0:T(8,128)(2,1)S(1)}, u32[]{:S(2)}, u32[]{:S(2)}) collective-permute-start(bf16[32,192]{1,0:T(8,128)(2,1)S(1)} %get-tuple-element.73), channel_id=1, source_target_pairs={{0,10},{1,11},{2,8},{3,9},{4,14},{5,15},{6,12},{7,13},{8,2},{9,3},... | collective-permute-start | bytes 36872 | tf_op jit(solution)/shard_map/ppermute | solution.py:24
  48.7 9.0 %collective-permute-start.16 = (bf16[32,192]{1,0:T(8,128)(2,1)S(1)}, bf16[32,192]{1,0:T(8,128)(2,1)S(1)}, u32[]{:S(2)}, u32[]{:S(2)}) collective-permute-start(bf16[32,192]{1,0:T(8,128)(2,1)S(1)} %get-tuple-element.72), channel_id=1, source_target_pairs={{0,11},{1,10},{2,9},{3,8},{4,15},{5,14},{6,13},{7,12},{8,3},{9,2},... | collective-permute-start | bytes 36872 | tf_op jit(solution)/shard_map/ppermute | solution.py:24
  49.8 8.0 %collective-permute-start.17 = (bf16[32,192]{1,0:T(8,128)(2,1)S(1)}, bf16[32,192]{1,0:T(8,128)(2,1)S(1)}, u32[]{:S(2)}, u32[]{:S(2)}) collective-permute-start(bf16[32,192]{1,0:T(8,128)(2,1)S(1)} %get-tuple-element.71), channel_id=1, source_target_pairs={{0,12},{1,13},{2,14},{3,15},{4,8},{5,9},{6,10},{7,11},{8,4},{9,5},... | collective-permute-start | bytes 36872 | tf_op jit(solution)/shard_map/ppermute | solution.py:24
  52.0 7.3 %collective-permute-start.18 = (bf16[32,192]{1,0:T(8,128)(2,1)S(1)}, bf16[32,192]{1,0:T(8,128)(2,1)S(1)}, u32[]{:S(2)}, u32[]{:S(2)}) collective-permute-start(bf16[32,192]{1,0:T(8,128)(2,1)S(1)} %get-tuple-element.70), channel_id=1, source_target_pairs={{0,13},{1,12},{2,15},{3,14},{4,9},{5,8},{6,11},{7,10},{8,5},{9,4},... | collective-permute-start | bytes 36872 | tf_op jit(solution)/shard_map/ppermute | solution.py:24
  52.7 6.7 %collective-permute-start.19 = (bf16[32,192]{1,0:T(8,128)(2,1)S(1)}, bf16[32,192]{1,0:T(8,128)(2,1)S(1)}, u32[]{:S(2)}, u32[]{:S(2)}) collective-permute-start(bf16[32,192]{1,0:T(8,128)(2,1)S(1)} %get-tuple-element.69), channel_id=1, source_target_pairs={{0,14},{1,15},{2,12},{3,13},{4,10},{5,11},{6,8},{7,9},{8,6},{9,7},... | collective-permute-start | bytes 36872 | tf_op jit(solution)/shard_map/ppermute | solution.py:24
  56.7 6.1 %collective-permute-start.20 = (bf16[32,192]{1,0:T(8,128)(2,1)S(1)}, bf16[32,192]{1,0:T(8,128)(2,1)S(1)}, u32[]{:S(2)}, u32[]{:S(2)}) collective-permute-start(bf16[32,192]{1,0:T(8,128)(2,1)S(1)} %get-tuple-element.68), channel_id=1, source_target_pairs={{0,15},{1,14},{2,13},{3,12},{4,11},{5,10},{6,9},{7,8},{8,7},{9,6},... | collective-permute-start | bytes 36872 | tf_op jit(solution)/shard_map/ppermute | solution.py:24
  57.8 11.2 %collective-permute-start.5 = (bf16[2,2,192,256]{3,2,1,0:T(8,128)(2,1)S(1)}, bf16[2,2,192,256]{3,2,1,0:T(8,128)(2,1)S(1)}, u32[]{:S(2)}, u32[]{:S(2)}) collective-permute-start(bf16[2,2,192,256]{3,2,1,0:T(8,128)(2,1)S(1)} %pad_maximum_fusion.10), channel_id=1, source_target_pairs={{0,4},{1,5},{2,6},{3,7},{4,0},{5,1},{6,2},{7,3},{8,12},{9,13},{10,... | collective-permute-start | bytes 1179656 | tf_op jit(solution)/shard_map/ppermute | solution.py:56
  57.8 11.3 %collective-permute-start.4 = (bf16[2,2,192,256]{3,2,0,1:T(8,128)(2,1)S(1)}, bf16[2,2,192,256]{3,2,0,1:T(8,128)(2,1)S(1)}, u32[]{:S(2)}, u32[]{:S(2)}) collective-permute-start(bf16[2,2,192,256]{3,2,0,1:T(8,128)(2,1)S(1)} %pad_maximum_fusion.9), channel_id=1, source_target_pairs={{0,2},{1,3},{2,0},{3,1},{4,6},{5,7},{6,4},{7,5},{8,10},{9,11},{10,... | collective-permute-start | bytes 1179656 | tf_op jit(solution)/shard_map/ppermute | solution.py:56
  69.0 1.2 copy-start.9
  71.3 7.1 %collective-permute-start.21 = (bf16[192,256]{1,0:T(8,128)(2,1)S(1)}, bf16[192,256]{1,0:T(8,128)(2,1)S(1)}, u32[]{:S(2)}, u32[]{:S(2)}) collective-permute-start(bf16[192,256]{1,0:T(8,128)(2,1)S(1)} %get-tuple-element.67), channel_id=1, source_target_pairs={{0,8},{1,9},{2,10},{3,11},{4,12},{5,13},{6,14},{7,15},{8,0},{9,1},... | collective-permute-start | bytes 294920 | tf_op jit(solution)/shard_map/ppermute | solution.py:56
  73.3 5.1 %collective-permute-start.22 = (bf16[192,256]{1,0:T(8,128)(2,1)S(1)}, bf16[192,256]{1,0:T(8,128)(2,1)S(1)}, u32[]{:S(2)}, u32[]{:S(2)}) collective-permute-start(bf16[192,256]{1,0:T(8,128)(2,1)S(1)} %get-tuple-element.66), channel_id=1, source_target_pairs={{0,2},{1,3},{2,0},{3,1},{4,6},{5,7},{6,4},{7,5},{8,10},{9,11},{10,... | collective-permute-start | bytes 294920 | tf_op jit(solution)/shard_map/ppermute | solution.py:56
  78.5 8.7 %collective-permute-start.23 = (bf16[2,192,256]{2,1,0:T(8,128)(2,1)S(1)}, bf16[2,192,256]{2,1,0:T(8,128)(2,1)S(1)}, u32[]{:S(2)}, u32[]{:S(2)}) collective-permute-start(bf16[2,192,256]{2,1,0:T(8,128)(2,1)S(1)} %pad_maximum_fusion.15), channel_id=1, source_target_pairs={{0,4},{1,5},{2,6},{3,7},{4,0},{5,1},{6,2},{7,3},{8,12},{9,13},{10,... | collective-permute-start | bytes 589832 | tf_op jit(solution)/shard_map/ppermute | solution.py:56
  79.6 24.1 %collective-permute-start.29 = (bf16[2,2,2,192,256]{4,3,0,1,2:T(8,128)(2,1)S(1)}, bf16[2,2,2,192,256]{4,3,0,1,2:T(8,128)(2,1)S(1)}, u32[]{:S(2)}, u32[]{:S(2)}) collective-permute-start(bf16[2,2,2,192,256]{4,3,0,1,2:T(8,128)(2,1)S(1)} %pad_maximum_fusion.5), channel_id=1, source_target_pairs={{0,1},{1,0},{2,3},{3,2},{4,5},{5,4},{6,7},{7,6},{8,9},{9,8},{10,11... | collective-permute-start | bytes 2359304 | tf_op jit(solution)/shard_map/ppermute | solution.py:56
  79.7 12.8 %collective-permute-start.26 = (bf16[2,192,256]{2,1,0:T(8,128)(2,1)S(1)}, bf16[2,192,256]{2,1,0:T(8,128)(2,1)S(1)}, u32[]{:S(2)}, u32[]{:S(2)}) collective-permute-start(bf16[2,192,256]{2,1,0:T(8,128)(2,1)S(1)} %pad_maximum_fusion.16), channel_id=1, source_target_pairs={{0,8},{1,9},{2,10},{3,11},{4,12},{5,13},{6,14},{7,15},{8,0},{9,1},... | collective-permute-start | bytes 589832 | tf_op jit(solution)/shard_map/ppermute | solution.py:56
  87.3 7.8 %collective-permute-start.24 = (bf16[2,2,192,256]{3,2,0,1:T(8,128)(2,1)S(1)}, bf16[2,2,192,256]{3,2,0,1:T(8,128)(2,1)S(1)}, u32[]{:S(2)}, u32[]{:S(2)}) collective-permute-start(bf16[2,2,192,256]{3,2,0,1:T(8,128)(2,1)S(1)} %pad_maximum_fusion.11), channel_id=1, source_target_pairs={{0,2},{1,3},{2,0},{3,1},{4,6},{5,7},{6,4},{7,5},{8,10},{9,11},{10,... | collective-permute-start | bytes 1179656 | tf_op jit(solution)/shard_map/ppermute | solution.py:56
  92.5 10.9 %collective-permute-start.27 = (bf16[2,2,192,256]{3,2,1,0:T(8,128)(2,1)S(1)}, bf16[2,2,192,256]{3,2,1,0:T(8,128)(2,1)S(1)}, u32[]{:S(2)}, u32[]{:S(2)}) collective-permute-start(bf16[2,2,192,256]{3,2,1,0:T(8,128)(2,1)S(1)} %pad_maximum_fusion.12), channel_id=1, source_target_pairs={{0,4},{1,5},{2,6},{3,7},{4,0},{5,1},{6,2},{7,3},{8,12},{9,13},{10,... | collective-permute-start | bytes 1179656 | tf_op jit(solution)/shard_map/ppermute | solution.py:56
  93.0 11.1 %collective-permute-start.30 = (bf16[2,2,2,192,256]{4,3,2,0,1:T(8,128)(2,1)S(1)}, bf16[2,2,2,192,256]{4,3,2,0,1:T(8,128)(2,1)S(1)}, u32[]{:S(2)}, u32[]{:S(2)}) collective-permute-start(bf16[2,2,2,192,256]{4,3,2,0,1:T(8,128)(2,1)S(1)} %pad_maximum_fusion.6), channel_id=1, source_target_pairs={{0,1},{1,0},{2,3},{3,2},{4,5},{5,4},{6,7},{7,6},{8,9},{9,8},{10,11... | collective-permute-start | bytes 2359304 | tf_op jit(solution)/shard_map/ppermute | solution.py:56
  95.3 11.8 %collective-permute-start.25 = (bf16[2,2,2,192,256]{4,3,0,1,2:T(8,128)(2,1)S(1)}, bf16[2,2,2,192,256]{4,3,0,1,2:T(8,128)(2,1)S(1)}, u32[]{:S(2)}, u32[]{:S(2)}) collective-permute-start(bf16[2,2,2,192,256]{4,3,0,1,2:T(8,128)(2,1)S(1)} %pad_maximum_fusion.7), channel_id=1, source_target_pairs={{0,1},{1,0},{2,3},{3,2},{4,5},{5,4},{6,7},{7,6},{8,9},{9,8},{10,11... | collective-permute-start | bytes 2359304 | tf_op jit(solution)/shard_map/ppermute | solution.py:56
  103.6 3.8 %collective-permute-start.28 = (bf16[2,2,2,192,256]{4,3,2,0,1:T(8,128)(2,1)S(1)}, bf16[2,2,2,192,256]{4,3,2,0,1:T(8,128)(2,1)S(1)}, u32[]{:S(2)}, u32[]{:S(2)}) collective-permute-start(bf16[2,2,2,192,256]{4,3,2,0,1:T(8,128)(2,1)S(1)} %pad_maximum_fusion.8), channel_id=1, source_target_pairs={{0,1},{1,0},{2,3},{3,2},{4,5},{5,4},{6,7},{7,6},{8,9},{9,8},{10,11... | collective-permute-start | bytes 2359304 | tf_op jit(solution)/shard_map/ppermute | solution.py:56
  104.5 1.6 %copy-start.4 = (bf16[1024,512]{1,0:T(8,128)(2,1)S(1)}, bf16[1024,512]{1,0:T(8,128)(2,1)}, u32[]{:S(2)}) copy-start(bf16[1024,512]{1,0:T(8,128)(2,1)} %param.9) | copy-start | bytes 3145732
  104.5 1.6 %copy-start.10 = (f32[192,512]{1,0:T(8,128)S(1)}, f32[192,512]{1,0:T(8,128)}, u32[]{:S(2)}) copy-start(f32[192,512]{1,0:T(8,128)} %get-tuple-element.89) | copy-start | bytes 1179652
  107.7 1.1 copy-start.6
  110.0 0.8 copy-start.7
  111.1 1.3 copy-start.1
  113.6 3.1 %collective-permute-start.31 = (f32[2,2,2,2,64,256]{5,4,3,2,1,0:T(8,128)}, f32[2,2,2,2,64,256]{5,4,3,2,1,0:T(8,128)}, u32[]{:S(2)}, u32[]{:S(2)}) collective-permute-start(f32[2,2,2,2,64,256]{5,4,3,2,1,0:T(8,128)} %dynamic-slice_bitcast_fusion), channel_id=1, source_target_pairs={{0,1},{1,0},{2,3},{3,2},{4,5},{5,4},{6,7},{7,6},{8,9},{9,8},{10,11... | collective-permute-start | bytes 3145736 | tf_op jit(solution)/shard_map/weight_grad_sum/ppermute | solution.py:56
  114.2 2.5 %copy-start.2 = (f32[2048,256]{1,0:T(8,128)S(1)}, f32[2048,256]{1,0:T(8,128)}, u32[]{:S(2)}) copy-start(f32[2048,256]{1,0:T(8,128)} %copy-done.1) | copy-start | bytes 6291460
  115.3 4.4 %collective-permute-start.36 = (f32[2,2,2,2,64,256]{5,4,2,1,0,3:T(8,128)}, f32[2,2,2,2,64,256]{5,4,2,1,0,3:T(8,128)}, u32[]{:S(2)}, u32[]{:S(2)}) collective-permute-start(f32[2,2,2,2,64,256]{5,4,2,1,0,3:T(8,128)} %bitcast.141), channel_id=1, source_target_pairs={{0,1},{1,0},{2,3},{3,2},{4,5},{5,4},{6,7},{7,6},{8,9},{9,8},{10,11... | collective-permute-start | bytes 3145736 | tf_op jit(solution)/shard_map/weight_grad_sum/ppermute | solution.py:56
  118.1 14.3 %collective-permute-start.32 = (f32[2,2,2,64,256]{4,3,2,1,0:T(8,128)S(1)}, f32[2,2,2,64,256]{4,3,2,1,0:T(8,128)S(1)}, u32[]{:S(2)}, u32[]{:S(2)}) collective-permute-start(f32[2,2,2,64,256]{4,3,2,1,0:T(8,128)S(1)} %dynamic-slice_bitcast_fusion.2), channel_id=1, source_target_pairs={{0,16},{16,0},{1,17},{17,1},{2,18},{18,2},{3,19},{19,3},{4,20},{20... | collective-permute-start | bytes 1572872 | tf_op jit(solution)/shard_map/weight_grad_sum/ppermute | solution.py:56
  119.7 3.1 %copy-start.5 = (bf16[1024,512]{1,0:T(8,128)(2,1)S(1)}, bf16[1024,512]{1,0:T(8,128)(2,1)}, u32[]{:S(2)}) copy-start(bf16[1024,512]{1,0:T(8,128)(2,1)} %param.9) | copy-start | bytes 3145732
  119.7 3.1 %copy-start.8 = (bf16[192,512]{1,0:T(8,128)(2,1)S(1)}, bf16[192,512]{1,0:T(8,128)(2,1)}, u32[]{:S(2)}) copy-start(bf16[192,512]{1,0:T(8,128)(2,1)} %copy-done.7) | copy-start | bytes 589828
  121.2 14.4 %collective-permute-start.37 = (f32[2,2,2,64,256]{4,3,2,1,0:T(8,128)S(1)}, f32[2,2,2,64,256]{4,3,2,1,0:T(8,128)S(1)}, u32[]{:S(2)}, u32[]{:S(2)}) collective-permute-start(f32[2,2,2,64,256]{4,3,2,1,0:T(8,128)S(1)} %dynamic-slice_bitcast_fusion.1), channel_id=1, source_target_pairs={{0,2},{1,3},{2,0},{3,1},{4,6},{5,7},{6,4},{7,5},{8,10},{9,11},{10,... | collective-permute-start | bytes 1572872 | tf_op jit(solution)/shard_map/weight_grad_sum/ppermute | solution.py:56
  132.5 8.3 %collective-permute-start.33 = (f32[2,2,64,256]{3,2,1,0:T(8,128)S(1)}, f32[2,2,64,256]{3,2,1,0:T(8,128)S(1)}, u32[]{:S(2)}, u32[]{:S(2)}) collective-permute-start(f32[2,2,64,256]{3,2,1,0:T(8,128)S(1)} %dynamic-slice_bitcast_fusion.4), channel_id=1, source_target_pairs={{0,2},{1,3},{2,0},{3,1},{4,6},{5,7},{6,4},{7,5},{8,10},{9,11},{10,... | collective-permute-start | bytes 786440 | tf_op jit(solution)/shard_map/weight_grad_sum/ppermute | solution.py:56
  135.7 7.3 %collective-permute-start.38 = (f32[2,2,64,256]{3,2,1,0:T(8,128)S(1)}, f32[2,2,64,256]{3,2,1,0:T(8,128)S(1)}, u32[]{:S(2)}, u32[]{:S(2)}) collective-permute-start(f32[2,2,64,256]{3,2,1,0:T(8,128)S(1)} %dynamic-slice_bitcast_fusion.3), channel_id=1, source_target_pairs={{0,16},{16,0},{1,17},{17,1},{2,18},{18,2},{3,19},{19,3},{4,20},{20... | collective-permute-start | bytes 786440 | tf_op jit(solution)/shard_map/weight_grad_sum/ppermute | solution.py:56
  140.9 8.1 %collective-permute-start.34 = (f32[2,64,256]{2,1,0:T(8,128)S(1)}, f32[2,64,256]{2,1,0:T(8,128)S(1)}, u32[]{:S(2)}, u32[]{:S(2)}) collective-permute-start(f32[2,64,256]{2,1,0:T(8,128)S(1)} %dynamic-slice_bitcast_fusion.6), channel_id=1, source_target_pairs={{0,8},{1,9},{2,10},{3,11},{4,12},{5,13},{6,14},{7,15},{8,0},{9,1},... | collective-permute-start | bytes 393224 | tf_op jit(solution)/shard_map/weight_grad_sum/ppermute | solution.py:56
  143.0 6.7 %collective-permute-start.39 = (f32[2,64,256]{2,1,0:T(8,128)S(1)}, f32[2,64,256]{2,1,0:T(8,128)S(1)}, u32[]{:S(2)}, u32[]{:S(2)}) collective-permute-start(f32[2,64,256]{2,1,0:T(8,128)S(1)} %dynamic-slice_bitcast_fusion.5), channel_id=1, source_target_pairs={{0,4},{1,5},{2,6},{3,7},{4,0},{5,1},{6,2},{7,3},{8,12},{9,13},{10,... | collective-permute-start | bytes 393224 | tf_op jit(solution)/shard_map/weight_grad_sum/ppermute | solution.py:56
  149.0 4.5 %collective-permute-start.35 = (f32[64,256]{1,0:T(8,128)S(1)}, f32[64,256]{1,0:T(8,128)S(1)}, u32[]{:S(2)}, u32[]{:S(2)}) collective-permute-start(f32[64,256]{1,0:T(8,128)S(1)} %dynamic-slice_bitcast_fusion.8), channel_id=1, source_target_pairs={{0,4},{1,5},{2,6},{3,7},{4,0},{5,1},{6,2},{7,3},{8,12},{9,13},{10,... | collective-permute-start | bytes 196616 | tf_op jit(solution)/shard_map/weight_grad_sum/ppermute | solution.py:56
  149.7 5.2 %collective-permute-start.40 = (f32[64,256]{1,0:T(8,128)S(1)}, f32[64,256]{1,0:T(8,128)S(1)}, u32[]{:S(2)}, u32[]{:S(2)}) collective-permute-start(f32[64,256]{1,0:T(8,128)S(1)} %dynamic-slice_bitcast_fusion.7), channel_id=1, source_target_pairs={{0,8},{1,9},{2,10},{3,11},{4,12},{5,13},{6,14},{7,15},{8,0},{9,1},... | collective-permute-start | bytes 196616 | tf_op jit(solution)/shard_map/weight_grad_sum/ppermute | solution.py:56
